TPU v7x, 512 devices: a whole 4x8x8 slice. The times are simulated.
512 devices in a mesh: lat: 32 (over z, x), lon: 16 (over y, core).
Axes of the slice: x: 4, y: 8, z: 8, core: 2. Of those that a mesh axis runs over, the one named last changes fastest.
Arguments:
- grid: bfloat16 [144, 128, 5136], P(None, 'lat', 'lon'), may hold values from -6 to 6
- cubic_weights: float32 [4, 128, 5136], P(None, 'lat', 'lon'), as said below
- dep_base: int32 [128, 5136], P('lat', 'lon'), may hold values from -2 to 128, as said below
- row_points: int32 [128], P('lat'), may hold values from 20 to 5136, as said below
- wave_order: int32 [640], replicated, may hold values from 0 to 639, each once
- legendre: bfloat16 [640, 128, 640], P('lat'), may hold values from -24 to 24
Outputs:
- spectral: bfloat16 [640, 144, 2, 640], P('lat', 'lon')
Inputs may be any that keep to these rules, and one draw needn't show every extreme that they name: dep_base[r, j] - r is one of -2, -1, 0, 1. `row_points`: every entry is 20 + 4 i for a whole number i. `cubic_weights`: the four weights of a point are the cubic Lagrange weights at nodes -1, 0, 1, 2 for one fraction in 0 to 1.
All inputs are finite; a program needn't handle non-finite values.
Results may differ from a plain program's by a relative error of at most 0.0062.
Values may be sent and summed in bfloat16 or wider, within the bound.
No kernel may reach another device: no remote copies, remote signals or barrier semaphores. Data moves between devices by JAX's collectives and lax.ppermute only.
A program may use at most 64 MiB of HBM per device.

v0:
```python
import math

import jax
import jax.numpy as jnp
from jax import lax
from jax.sharding import PartitionSpec as P

M = 640
NDEG = 640
HALO = 3


def extended(block, sides, width):
    for axis, dim in sides:
        count = lax.axis_size(axis)
        forward = [(i, i + 1) for i in range(count - 1)]
        backward = [(target, source) for source, target in forward]
        low = lax.ppermute(
            lax.slice_in_dim(block, block.shape[dim] - width, None, axis=dim), axis, forward
        )
        high = lax.ppermute(lax.slice_in_dim(block, 0, width, axis=dim), axis, backward)
        block = jnp.concatenate([low, block, high], axis=dim)
    return block


def segment_tables(points, seg_len, waves):
    wavenumber = jnp.arange(waves, dtype=jnp.int32)
    position = jnp.arange(seg_len, dtype=jnp.int32)
    product = position[None, :, None] * wavenumber[None, None, :] % points[:, None, None]
    angles = 2.0 * math.pi * product.astype(jnp.float32) / points[:, None, None].astype(jnp.float32)
    return jnp.concatenate([jnp.cos(angles), -jnp.sin(angles)], axis=2).astype(jnp.bfloat16)


def phase_pair(points, starts, waves):
    wavenumber = jnp.arange(waves, dtype=jnp.int32)
    shifted = starts[None, :] % points[:, None]
    product = shifted[:, :, None] * wavenumber[None, None, :] % points[:, None, None]
    angles = 2.0 * math.pi * product.astype(jnp.float32) / points[:, None, None].astype(jnp.float32)
    return (jnp.cos(angles), -jnp.sin(angles))


def shards(grid, cubic_weights, dep_base, row_points, wave_order, legendre):
    columns, band_rows, seg_len = grid.shape
    pieces = lax.axis_size("lon")
    slots = legendre.shape[0]
    first_row = lax.axis_index("lat") * band_rows
    first_point = lax.axis_index("lon") * seg_len
    padded = extended(grid, (("lat", 1),), HALO)
    offset = dep_base - (first_row + jnp.arange(band_rows, dtype=jnp.int32))[:, None]
    arrival = jnp.zeros((columns, band_rows, seg_len), jnp.float32)
    for displace in range(-HALO, HALO + 1):
        stencil = jnp.zeros((band_rows, seg_len), jnp.float32)
        for node in range(4):
            stencil = stencil + jnp.where(
                offset - 1 + node == displace, cubic_weights[node], jnp.float32(0.0)
            )
        arrival = arrival + stencil[None] * padded[
            :, HALO + displace : HALO + displace + band_rows, :
        ].astype(jnp.float32)
    inside = (first_point + jnp.arange(seg_len, dtype=jnp.int32))[None, :] < row_points[:, None]
    arrival = jnp.where(inside[None], arrival, jnp.float32(0.0)).astype(jnp.bfloat16)
    tables = segment_tables(row_points, seg_len, M)
    own_start = jnp.reshape(first_point, (1,))
    phase_re, phase_im = phase_pair(row_points, own_start, M)
    spectra = jnp.einsum("crj,rjx->crx", arrival, tables, preferred_element_type=jnp.float32)
    spectra = spectra.reshape(columns // pieces * lax.axis_size("lon"), band_rows, 2, M)
    real_part = (
        phase_re[None, :, 0, :] * spectra[:, :, 0] - phase_im[None, :, 0, :] * spectra[:, :, 1]
    )
    imag_part = (
        phase_re[None, :, 0, :] * spectra[:, :, 1] + phase_im[None, :, 0, :] * spectra[:, :, 0]
    )
    fourier = lax.psum_scatter(
        jnp.stack([real_part, imag_part], axis=2), "lon", scatter_dimension=0, tiled=True
    )
    wavenumber = jnp.arange(M, dtype=jnp.int32)
    inverse = jnp.float32(1.0) / row_points.astype(jnp.float32)
    resolved = 2 * wavenumber[None, :] < row_points[:, None]
    fourier = jnp.where(
        resolved[None, :, None, :], fourier * inverse[None, :, None, None], jnp.float32(0.0)
    )
    fourier = fourier.astype(jnp.bfloat16)
    sorted_waves = jnp.take(fourier, wave_order, axis=3)
    my_slots = lax.dynamic_slice_in_dim(wave_order, lax.axis_index("lat") * slots, slots)
    degree = jnp.arange(NDEG, dtype=jnp.int32)
    masked_table = jnp.where(
        degree[None, None, :] >= my_slots[:, None, None], legendre, jnp.zeros((), legendre.dtype)
    )
    result = jnp.einsum(
        "clts,sln->sctn",
        lax.all_to_all(sorted_waves, "lat", split_axis=3, concat_axis=1, tiled=True),
        masked_table,
        preferred_element_type=jnp.float32,
    )
    return result.astype(jnp.bfloat16)


def solution(mesh):
    return jax.shard_map(
        shards,
        mesh=mesh,
        in_specs=(
            P(None, "lat", "lon"),
            P(None, "lat", "lon"),
            P("lat", "lon"),
            P("lat"),
            P(),
            P("lat", None, None),
        ),
        out_specs=P("lat", "lon", None, None),
        check_vma=False,
    )
```

profile of v0, /device:TPU:1, one launch (start us, length us, event | category | flops | bytes accessed | tf_op | source)
XLA Modules:
  0.0 248.2 jit_solution(10175704246700488639)
XLA Ops:
  6.5 0.0 copy-start.4
  6.5 0.0 all-reduce.3.cloned.1.call-start
  6.5 1.6 fusion.55
  8.1 4.0 %collective-permute-start = (bf16[144,3,321]{2,1,0:T(4,128)(2,1)S(1)}, bf16[144,3,321]{2,1,0:T(4,128)(2,1)S(1)}, u32[]{:S(2)}, u32[]{:S(2)}) collective-permute-start(bf16[144,3,321]{2,1,0:T(4,128)(2,1)S(1)} %get-tuple-element.11), channel_id=1, source_target_pairs={{0,16},{16,32},{32,48},{48,64},{64,80},{80,96},{96,112},{112,128},... | collective-permute-start | bytes 832040 | tf_op jit(solution)/shard_map/ppermute | solution.py:18
  12.1 1.3 collective-permute-start.1
  13.4 0.0 copy-done.4
  13.4 0.1 and_select_fusion
  13.6 0.1 iota_multiply_fusion
  13.6 0.0 copy-start.1
  13.7 0.0 copy-start.2
  13.7 0.0 copy-start
  13.7 44.3 %cosine_convert_fusion = (bf16[4,321,640]{2,1,0:T(8,128)(2,1)S(1)}, bf16[4,321,640]{2,1,0:T(8,128)(2,1)S(1)}) fusion(f32[4]{0:T(128)S(1)} %get-tuple-element.24, pred[4]{0:T(512)(128)(4,1)S(1)} %broadcast_compare_fusion.2, s32[4]{0:T(128)S(1)} %get-tuple-element.23, s32[321,640]{1,0:T(8,128)S(1)} %iota_multiply_fusion), kind=kLoop, calls=%fused_computation.13 | loop fusion | flops 10682880 | bytes 4108836 | tf_op jit(solution)/shard_map/convert
  58.0 0.4 fusion.51
  58.4 0.0 copy-done.1
  58.4 0.0 copy-done.2
  58.4 0.1 fusion.34
  58.5 0.1 broadcast_compare_fusion.1
  58.6 0.1 fusion.30
  58.7 0.0 collective-permute-done
  58.7 0.0 collective-permute-done.1
  58.7 0.0 copy-done
  58.7 3.2 %select_convert_fusion = bf16[144,4,321]{2,1,0:T(4,128)(2,1)S(1)} fusion(bf16[144,4,321]{2,1,0:T(4,128)(2,1)S(1)} %copy-done, bf16[144,3,321]{2,1,0:T(4,128)(2,1)S(1)} %collective-permute-done.1, bf16[144,3,321]{2,1,0:T(4,128)(2,1)S(1)} %collective-permute-done, f32[4,321]{1,0:T(4,128)S(1)} %get-tuple-element.19, f32[4,321]{1,0:T(4,128)S(1)} %get-tuple-element.18, ...), kind=kLoop, calls=%fused_computation.34 | loop fusion | flops 7395840 | bytes 1331508 | tf_op jit(solution)/shard_map/convert_element_type | solution.py:61
  61.9 2.5 %convolution_bitcast_fusion = f32[144,4,1280]{2,0,1:T(8,128)} fusion(bf16[4,321,640]{2,1,0:T(8,128)(2,1)S(1)} %get-tuple-element.10, bf16[4,321,640]{2,1,0:T(8,128)(2,1)S(1)} %get-tuple-element.9, bf16[144,4,321]{2,1,0:T(4,128)(2,1)S(1)} %select_convert_fusion), kind=kOutput, calls=%fused_computation.5 | convolution fusion | flops 479907840 | bytes 6605952 | tf_op jit(solution)/shard_map/crj,rjx->crx/dot_general | solution.py:65
  64.4 3.4 %reshape.292 = f32[144,4,2,640]{3,2,0,1:T(2,128)S(1)} reshape(f32[144,4,1280]{2,0,1:T(8,128)} %convolution_bitcast_fusion) | data formatting | bytes 5898240 | tf_op jit(solution)/shard_map/reshape | solution.py:66
  67.9 2.3 fusion.54
  70.1 1.2 multiply_subtract_fusion
  71.3 2.2 pad_maximum_fusion
  73.5 0.0 copy-start.3
  73.5 0.0 all-reduce.3.cloned.1.call-update
  73.6 1.3 dynamic-slice
  75.5 0.0 copy-done.3
  75.5 0.1 dynamic_slice.3
  75.6 0.1 broadcast_compare_fusion
  75.7 127.9 %all-reduce.3.cloned.1.call-done = f32[144,4,2,640]{3,1,2,0:T(4,128)} async-done(((f32[144,4,2,640]{3,1,2,0:T(4,128)}), f32[144,4,2,640]{3,1,2,0:T(4,128)}) %all-reduce.3.cloned.1.call-update) | async-done | bytes 2949136
  203.6 1.0 fusion.22
  204.6 0.9 copy.31
  205.5 3.5 %gather_fusion = bf16[640,9,4,2]{1,2,3,0:T(4,128)(2,1)S(1)} fusion(bf16[9,4,2,640]{0,1,3,2:T(4,128)(2,1)S(1)} %copy.31, s32[1024]{0:T(1024)S(1)} %pad_clamp_fusion), kind=kCustom, calls=%fused_computation | custom fusion | bytes 186880 | tf_op jit(solution)/shard_map/jit(_take)/gather | solution.py:83
  209.1 2.3 fusion.56
  211.4 2.0 reshape.304
  213.4 10.1 %all-to-all-start = ((bf16[32,2,720]{2,1,0:T(2,128)(2,1)}), bf16[32,2,720]{2,1,0:T(2,128)(2,1)S(1)}, u32[]{:S(2)}, u32[]{:S(2)}) async-start(bf16[32,2,720]{2,1,0:T(2,128)(2,1)} %reshape.304), calls=%async_computation | async-start | bytes 196608 | tf_op jit(solution)/shard_map/all_to_all | solution.py:91
  223.6 0.1 iota_compare_fusion
  223.7 8.8 %all-to-all-done = bf16[32,2,720]{2,1,0:T(2,128)(2,1)S(1)} async-done(((bf16[32,2,720]{2,1,0:T(2,128)(2,1)}), bf16[32,2,720]{2,1,0:T(2,128)(2,1)S(1)}, u32[]{:S(2)}, u32[]{:S(2)}) %all-to-all-start) | async-done | bytes 92192 | tf_op jit(solution)/shard_map/all_to_all | solution.py:91
  232.4 1.6 reshape.305
  234.0 2.7 %copy.37 = bf16[9,4,2,32,20]{4,3,2,1,0:T(8,128)(2,1)S(1)} copy(bf16[9,4,2,32,20]{0,1,2,4,3:T(4,128)(2,1)S(1)} %bitcast.139) | data formatting | bytes 184320 | tf_op jit(solution)/shard_map/all_to_all | solution.py:91
  236.7 0.5 copy.33
  237.2 0.5 copy.34
  237.6 2.6 %fusion.13 = bf16[20,9,2,640]{3,1,2,0:T(8,128)(2,1)S(1)} fusion(bf16[9,128,2,20]{1,0,2,3:T(8,128)(2,1)S(1)} %copy.34, bf16[20,128,640]{2,1,0:T(8,128)(2,1)} %param.11, pred[20,640]{1,0:T(8,128)(4,1)S(1)} %iota_compare_fusion), kind=kOutput, calls=%fused_computation.24 | convolution fusion | flops 60851200 | bytes 3842560 | tf_op jit(solution)/shard_map/clts,sln->sctn/dot_general | solution.py:89
  240.2 1.1 copy.35
  (8 shorter events, 0.0 us)
Async XLA Ops:
  6.5 6.9 %copy-start.4 = (s32[4]{0:T(128)S(1)}, s32[4]{0:T(128)}, u32[]{:S(2)}) copy-start(s32[4]{0:T(128)} %param.9) | copy-start | bytes 52
  6.5 197.0 %all-reduce.3.cloned.1.call-start = ((), (), s32[]{:S(2)}) async-start(), calls=%async_computation.1 | async-start | bytes 5898240
  8.1 50.5 %collective-permute-start = (bf16[144,3,321]{2,1,0:T(4,128)(2,1)S(1)}, bf16[144,3,321]{2,1,0:T(4,128)(2,1)S(1)}, u32[]{:S(2)}, u32[]{:S(2)}) collective-permute-start(bf16[144,3,321]{2,1,0:T(4,128)(2,1)S(1)} %get-tuple-element.11), channel_id=1, source_target_pairs={{0,16},{16,32},{32,48},{48,64},{64,80},{80,96},{96,112},{112,128},... | collective-permute-start | bytes 832040 | tf_op jit(solution)/shard_map/ppermute | solution.py:18
  12.1 46.6 %collective-permute-start.1 = (bf16[144,3,321]{2,1,0:T(4,128)(2,1)S(1)}, bf16[144,3,321]{2,1,0:T(4,128)(2,1)S(1)}, u32[]{:S(2)}, u32[]{:S(2)}) collective-permute-start(bf16[144,3,321]{2,1,0:T(4,128)(2,1)S(1)} %get-tuple-element.12), channel_id=1, source_target_pairs={{16,0},{32,16},{48,32},{64,48},{80,64},{96,80},{112,96},{128,112},... | collective-permute-start | bytes 832040 | tf_op jit(solution)/shard_map/ppermute | solution.py:21
  13.6 44.7 %copy-start.1 = (f32[4,4,321]{2,1,0:T(4,128)S(1)}, f32[4,4,321]{2,1,0:T(4,128)}, u32[]{:S(2)}) copy-start(f32[4,4,321]{2,1,0:T(4,128)} %param.7) | copy-start | bytes 61636
  13.7 44.7 %copy-start.2 = (s32[4,321]{1,0:T(4,128)S(1)}, s32[4,321]{1,0:T(4,128)}, u32[]{:S(2)}) copy-start(s32[4,321]{1,0:T(4,128)} %param.8) | copy-start | bytes 15412
  13.7 45.0 %copy-start = (bf16[144,4,321]{2,1,0:T(4,128)(2,1)S(1)}, bf16[144,4,321]{2,1,0:T(4,128)(2,1)}, u32[]{:S(2)}) copy-start(bf16[144,4,321]{2,1,0:T(4,128)(2,1)} %param.6) | copy-start | bytes 1109380
  73.5 2.0 copy-start.3
  213.4 19.0 %all-to-all-start = ((bf16[32,2,720]{2,1,0:T(2,128)(2,1)}), bf16[32,2,720]{2,1,0:T(2,128)(2,1)S(1)}, u32[]{:S(2)}, u32[]{:S(2)}) async-start(bf16[32,2,720]{2,1,0:T(2,128)(2,1)} %reshape.304), calls=%async_computation | async-start | bytes 196608 | tf_op jit(solution)/shard_map/all_to_all | solution.py:91
Sparse Core Ops, SparseCore 0:
  73.7 129.8 all-reduce.2
where the time goes:
time: 250 us; the launch traced here: 248 us
  waiting for transfers between devices  137 us (55%)
  other arithmetic  55.3 us (22%)
  local copies, waits for them, and re-layouts  21.4 us (9%)
  starting transfers between devices  15.4 us (6%)
  between operations  14.3 us (6%)
  matrix products  5.12 us (2%)
    unnamed x2, waiting for transfers between devices  128 us
    another operation x1, other arithmetic  44.3 us
    all_to_all x1, starting transfers between devices, shards(): lax.all_to_all(sorted_waves, 'lat', split_axis=3, concat_axis=1, tiled=True)  10.1 us
    all_to_all x1, waiting for transfers between devices, shards(): lax.all_to_all(sorted_waves, 'lat', split_axis=3, concat_axis=1, tiled=True)  8.78 us
  transfers between devices with their start and end apart: 4, of which 2 were waited for; matrix products, arithmetic and copies ran while one was open for 19% of the time, Pallas kernels for 0%

commit v1 on v0

--- a/solution.py
+++ b/solution.py
@@ -8,6 +8,7 @@
 M = 640
 NDEG = 640
 HALO = 3
+SPLIT = 64
 
 
 def extended(block, sides, width):
@@ -23,12 +24,21 @@
     return block
 
 
+def angles_of(points, position, wavenumber):
+    product = position[None, :, None] * wavenumber[None, None, :] % points[:, None, None]
+    return 2.0 * math.pi * product.astype(jnp.float32) / points[:, None, None].astype(jnp.float32)
+
+
 def segment_tables(points, seg_len, waves):
-    wavenumber = jnp.arange(waves, dtype=jnp.int32)
     position = jnp.arange(seg_len, dtype=jnp.int32)
-    product = position[None, :, None] * wavenumber[None, None, :] % points[:, None, None]
-    angles = 2.0 * math.pi * product.astype(jnp.float32) / points[:, None, None].astype(jnp.float32)
-    return jnp.concatenate([jnp.cos(angles), -jnp.sin(angles)], axis=2).astype(jnp.bfloat16)
+    high = angles_of(points, position, jnp.arange(waves // SPLIT, dtype=jnp.int32) * SPLIT)
+    low = angles_of(points, position, jnp.arange(SPLIT, dtype=jnp.int32))
+    ch, sh = jnp.cos(high)[..., :, None], jnp.sin(high)[..., :, None]
+    cl, sl = jnp.cos(low)[..., None, :], jnp.sin(low)[..., None, :]
+    shape = (points.shape[0], seg_len, waves)
+    cosine = (ch * cl - sh * sl).reshape(shape)
+    sine = (sh * cl + ch * sl).reshape(shape)
+    return jnp.stack([cosine, -sine], axis=2).astype(jnp.bfloat16)
 
 
 def phase_pair(points, starts, waves):
@@ -42,6 +52,7 @@
 def shards(grid, cubic_weights, dep_base, row_points, wave_order, legendre):
     columns, band_rows, seg_len = grid.shape
     pieces = lax.axis_size("lon")
+    keep = columns // pieces
     slots = legendre.shape[0]
     first_row = lax.axis_index("lat") * band_rows
     first_point = lax.axis_index("lon") * seg_len
@@ -59,20 +70,22 @@
         ].astype(jnp.float32)
     inside = (first_point + jnp.arange(seg_len, dtype=jnp.int32))[None, :] < row_points[:, None]
     arrival = jnp.where(inside[None], arrival, jnp.float32(0.0)).astype(jnp.bfloat16)
+    gathered = lax.all_to_all(
+        arrival.reshape(pieces, keep, band_rows, seg_len), "lon", split_axis=0, concat_axis=0, tiled=True
+    )
     tables = segment_tables(row_points, seg_len, M)
-    own_start = jnp.reshape(first_point, (1,))
-    phase_re, phase_im = phase_pair(row_points, own_start, M)
-    spectra = jnp.einsum("crj,rjx->crx", arrival, tables, preferred_element_type=jnp.float32)
-    spectra = spectra.reshape(columns // pieces * lax.axis_size("lon"), band_rows, 2, M)
-    real_part = (
-        phase_re[None, :, 0, :] * spectra[:, :, 0] - phase_im[None, :, 0, :] * spectra[:, :, 1]
+    starts = jnp.arange(pieces, dtype=jnp.int32) * seg_len
+    phase_re, phase_im = phase_pair(row_points, starts, M)
+    spectra = jnp.einsum(
+        "pcrj,rjtx->rtpcx", gathered, tables, preferred_element_type=jnp.float32
     )
-    imag_part = (
-        phase_re[None, :, 0, :] * spectra[:, :, 1] + phase_im[None, :, 0, :] * spectra[:, :, 0]
+    real_part = jnp.sum(
+        phase_re[:, :, None, :] * spectra[:, 0] - phase_im[:, :, None, :] * spectra[:, 1], axis=1
     )
-    fourier = lax.psum_scatter(
-        jnp.stack([real_part, imag_part], axis=2), "lon", scatter_dimension=0, tiled=True
+    imag_part = jnp.sum(
+        phase_re[:, :, None, :] * spectra[:, 1] + phase_im[:, :, None, :] * spectra[:, 0], axis=1
     )
+    fourier = jnp.stack([real_part, imag_part], axis=2).transpose(1, 0, 2, 3)
     wavenumber = jnp.arange(M, dtype=jnp.int32)
     inverse = jnp.float32(1.0) / row_points.astype(jnp.float32)
     resolved = 2 * wavenumber[None, :] < row_points[:, None]

time: 250 us -> 96.4 us (0.39)
  waiting for transfers between devices: 137 us -> 16.5 us
  other arithmetic: 55.3 us -> 23.6 us
  between operations: 14.3 us -> 0.26 us
  starting transfers between devices: 15.4 us -> 28.6 us
    unnamed x2 -> x0, waiting for transfers between devices: 128 us -> none
    another operation x2 -> x1, other arithmetic: 46.5 us -> 2.75 us
    all_to_all x0 -> x1, starting transfers between devices: none -> 8.29 us  [shards(): lax.all_to_all(arrival.reshape(pieces, keep, band_rows, seg_len), 'lon',...]
    all_to_all x0 -> x1, waiting for transfers between devices: none -> 6.88 us  [shards(): lax.all_to_all(arrival.reshape(pieces, keep, band_rows, seg_len), 'lon',...]
    cos x0 -> x2, other arithmetic: none -> 6.6 us  [the longest x1 5.2 us: segment_tables(): cl, sl = (jnp.cos(low)[..., None, :], jnp.sin(low)[..., None, :])]
    all_to_all x1, starting transfers between devices: 10.1 us -> 14.4 us  [shards(): lax.all_to_all(sorted_waves, 'lat', split_axis=3, concat_axis=1, tiled=True)]
    sub x0 -> x1, local copies, waits for them, and re-layouts: none -> 3.89 us  [segment_tables(): cosine = (ch * cl - sh * sl).reshape(shape)]
    reshape x1 -> x0, local copies, waits for them, and re-layouts: 3.42 us -> none  [shards(): spectra.reshape(columns // pieces * lax.axis_size('lon'), band_rows, 2, M)]
  transfers between devices with their start and end apart: 4 -> 4, of which waited for: 2 -> 2; matrix products, arithmetic and copies ran while one was open for 19% -> 22% of each run, Pallas kernels for 0% -> 0%
where the time goes in v1:
time: 96.4 us; the launch traced here: 95.9 us
  starting transfers between devices  28.6 us (30%)
  other arithmetic  23.6 us (24%)
  local copies, waits for them, and re-layouts  21.6 us (22%)
  waiting for transfers between devices  16.5 us (17%)
  matrix products  5.44 us (6%)
    all_to_all x1, starting transfers between devices, shards(): lax.all_to_all(sorted_waves, 'lat', split_axis=3, concat_axis=1, tiled=True)  14.4 us
    all_to_all x1, waiting for transfers between devices, shards(): lax.all_to_all(sorted_waves, 'lat', split_axis=3, concat_axis=1, tiled=True)  9.59 us
    all_to_all x1, starting transfers between devices, shards(): lax.all_to_all(arrival.reshape(pieces, keep, band_rows, seg_len), 'lon',...  8.29 us
    all_to_all x1, waiting for transfers between devices, shards(): lax.all_to_all(arrival.reshape(pieces, keep, band_rows, seg_len), 'lon',...  6.88 us
    convert_element_type x1, other arithmetic, shards(): jnp.where(inside[None], arrival, jnp.float32(0.0)).astype(jnp.bfloat16)  5.95 us
    cos x1, other arithmetic, segment_tables(): cl, sl = (jnp.cos(low)[..., None, :], jnp.sin(low)[..., None, :])  5.2 us
    ppermute x1, starting transfers between devices, extended(): lax.ppermute(lax.slice_in_dim(block, block.shape[dim] - width, None, axis...  4.71 us
    sub x1, local copies, waits for them, and re-layouts, segment_tables(): cosine = (ch * cl - sh * sl).reshape(shape)  3.89 us
  transfers between devices with their start and end apart: 4, of which 2 were waited for; matrix products, arithmetic and copies ran while one was open for 22% of the time, Pallas kernels for 0%

profile of v1, /device:TPU:1, one launch (start us, length us, event | category | flops | bytes accessed | tf_op | source)
XLA Modules:
  0.0 95.9 jit_solution(3147768930547831620)
XLA Ops:
  0.0 0.0 copy-start.4
  0.0 0.0 copy-start.2
  0.0 2.3 %fusion.67 = (bf16[144,3,321]{2,1,0:T(4,128)(2,1)}, bf16[144,3,321]{2,1,0:T(4,128)(2,1)S(1)}) fusion(bf16[144,4,321]{2,1,0:T(4,128)(2,1)} %param.6), kind=kLoop, calls=%fused_computation.149 | loop fusion | bytes 1109376 | tf_op jit(solution)/shard_map/slice | solution.py:20
  2.4 4.7 %collective-permute-start = (bf16[144,3,321]{2,1,0:T(4,128)(2,1)}, bf16[144,3,321]{2,1,0:T(4,128)(2,1)}, u32[]{:S(2)}, u32[]{:S(2)}) collective-permute-start(bf16[144,3,321]{2,1,0:T(4,128)(2,1)} %get-tuple-element.9), channel_id=1, source_target_pairs={{0,16},{16,32},{32,48},{48,64},{64,80},{80,96},{96,112},{112,128},... | collective-permute-start | bytes 832040 | tf_op jit(solution)/shard_map/ppermute | solution.py:19
  7.1 1.3 %collective-permute-start.1 = (bf16[144,3,321]{2,1,0:T(4,128)(2,1)S(1)}, bf16[144,3,321]{2,1,0:T(4,128)(2,1)}, u32[]{:S(2)}, u32[]{:S(2)}) collective-permute-start(bf16[144,3,321]{2,1,0:T(4,128)(2,1)S(1)} %get-tuple-element.10), channel_id=1, source_target_pairs={{16,0},{32,16},{48,32},{64,48},{80,64},{96,80},{112,96},{128,112},... | collective-permute-start | bytes 832040 | tf_op jit(solution)/shard_map/ppermute | solution.py:22
  8.4 0.7 compare_select_fusion.1
  9.1 0.7 broadcast_compare_fusion.2
  9.8 0.7 broadcast_divide_fusion
  10.5 0.1 iota_multiply_fusion.1
  10.5 5.2 %fusion.23 = (f32[4,321,64]{1,2,0:T(8,128)S(1)}, f32[4,321,64]{1,2,0:T(8,128)S(1)}) fusion(f32[4]{0:T(128)S(1)} %get-tuple-element.25, pred[4]{0:T(512)(128)(4,1)S(1)} %broadcast_compare_fusion.2, s32[4]{0:T(128)S(1)} %get-tuple-element.24, s32[321,64]{0,1:T(8,128)S(1)} %iota_multiply_fusion), kind=kLoop, calls=%fused_computation.50 | loop fusion | flops 821760 | bytes 739620 | tf_op jit(solution)/shard_map/cos | solution.py:37
  15.7 1.4 %fusion.41 = (f32[4,321,10]{1,2,0:T(8,128)S(1)}, f32[4,321,10]{1,2,0:T(8,128)S(1)}) fusion(f32[4]{0:T(128)S(1)} %get-tuple-element.25, pred[4]{0:T(512)(128)(4,1)S(1)} %broadcast_compare_fusion.2, s32[4]{0:T(128)S(1)} %get-tuple-element.24, s32[321,10]{0,1:T(8,128)S(1)} %iota_multiply_fusion.1), kind=kLoop, calls=%fused_computation.73 | loop fusion | flops 128400 | bytes 115596 | tf_op jit(solution)/shard_map/cos | solution.py:36
  17.2 0.0 copy-done.4
  17.2 0.1 broadcast_compare_fusion.1
  17.2 0.2 remainder_select_fusion.2
  17.4 0.0 copy-done.3
  17.5 0.0 copy-done.1
  17.5 0.0 copy-done.2
  17.5 0.1 fusion.46
  17.6 0.0 copy-start
  17.6 2.7 %subtract_convert_fusion = (bf16[4,321,10,64]{1,3,2,0:T(8,128)(2,1)}, bf16[4,321,10,64]{1,3,2,0:T(8,128)(2,1)S(1)}) fusion(f32[4,321,64]{1,2,0:T(8,128)S(1)} %get-tuple-element.12, f32[4,321,10]{1,2,0:T(8,128)S(1)} %get-tuple-element.21, f32[4,321,64]{1,2,0:T(8,128)S(1)} %get-tuple-element.11, f32[4,321,10]{1,2,0:T(8,128)S(1)} %get-tuple-element.20), kind=kLoop, calls=%fused_computation.2 | loop fusion | flops 7395840 | bytes 4047168 | tf_op jit(solution)/shard_map/convert.3
  20.3 0.1 fusion.42
  20.4 0.0 collective-permute-done
  20.4 0.0 collective-permute-done.1
  20.5 0.0 copy-done
  20.5 5.9 %select_convert_fusion = bf16[144,4,321]{2,1,0:T(4,128)(2,1)} fusion(bf16[144,4,321]{2,1,0:T(4,128)(2,1)S(1)} %copy-done, bf16[144,3,321]{2,1,0:T(4,128)(2,1)} %collective-permute-done.1, bf16[144,3,321]{2,1,0:T(4,128)(2,1)} %collective-permute-done, f32[4,321]{1,0:T(4,128)S(1)} %get-tuple-element.19, f32[4,321]{1,0:T(4,128)S(1)} %get-tuple-element.18, ...), kind=kLoop, calls=%fused_computation.31 | loop fusion | flops 7395840 | bytes 1331508 | tf_op jit(solution)/shard_map/convert_element_type | solution.py:72
  26.4 8.3 %all-to-all-start = ((bf16[16,9,4,321]{3,2,1,0:T(4,128)(2,1)}), bf16[16,9,4,321]{3,2,1,0:T(4,128)(2,1)S(1)}, u32[]{:S(2)}, u32[]{:S(2)}) async-start(bf16[16,9,4,321]{3,2,1,0:T(4,128)(2,1)} %bitcast.8), calls=%async_computation | async-start | bytes 884736 | tf_op jit(solution)/shard_map/all_to_all | solution.py:73
  34.7 3.9 %copy.52 = bf16[4,321,1,640]{3,1,2,0:T(8,128)(2,1)} copy(bf16[4,321,1,640]{1,3,0,2:T(8,128)(2,1)} %bitcast.166) | data formatting | bytes 3287040 | tf_op jit(solution)/shard_map/sub | solution.py:39
  38.6 2.3 %copy.53 = bf16[4,321,1,640]{3,1,2,0:T(8,128)(2,1)} copy(bf16[4,321,1,640]{1,3,0,2:T(8,128)(2,1)S(1)} %bitcast.165) | data formatting | bytes 3287040 | tf_op jit(solution)/shard_map/neg | solution.py:41
  40.9 0.1 dynamic_slice.3
  41.0 0.1 broadcast_compare_fusion
  41.0 2.3 %fusion.39 = (f32[4,16,640]{2,1,0:T(8,128)S(1)}, f32[4,16,640]{2,1,0:T(8,128)S(1)}) fusion(f32[4]{0:T(128)S(1)} %get-tuple-element.25, pred[4]{0:T(512)(128)(4,1)S(1)} %broadcast_compare_fusion.2, s32[4]{0:T(128)S(1)} %get-tuple-element.24, s32[4,16]{1,0:T(4,128)S(1)} %remainder_select_fusion.2), kind=kLoop, calls=%fused_computation.70 | loop fusion | flops 491520 | bytes 327972 | tf_op jit(solution)/shard_map/cos | solution.py:49
  43.3 6.9 %all-to-all-done = bf16[16,9,4,321]{3,2,1,0:T(4,128)(2,1)S(1)} async-done(((bf16[16,9,4,321]{3,2,1,0:T(4,128)(2,1)}), bf16[16,9,4,321]{3,2,1,0:T(4,128)(2,1)S(1)}, u32[]{:S(2)}, u32[]{:S(2)}) %all-to-all-start) | async-done | bytes 369824 | tf_op jit(solution)/shard_map/all_to_all | solution.py:73
  50.2 2.9 %fusion.7 = f32[4,2,16,9,640]{4,2,3,1,0:T(8,128)S(1)} fusion(bf16[4,321,1,640]{3,1,2,0:T(8,128)(2,1)} %copy.53, bf16[4,321,1,640]{3,1,2,0:T(8,128)(2,1)} %copy.52, bf16[16,9,4,321,1]{3,2,1,0,4:T(4,128)(2,1)S(1)} %bitcast.172), kind=kOutput, calls=%fused_computation.11 | convolution fusion | flops 479907840 | bytes 6605952 | tf_op jit(solution)/shard_map/pcrj,rjtx->rtpcx/dot_general | solution.py:79
  53.1 0.8 subtract_reduce_fusion
  53.9 0.1 fusion.38
  54.1 0.9 copy.60
  55.0 3.5 %gather_fusion = bf16[640,9,4,2]{1,2,3,0:T(4,128)(2,1)S(1)} fusion(bf16[9,4,2,640]{0,1,3,2:T(4,128)(2,1)S(1)} %copy.60, s32[1024]{0:T(1024)S(1)} %pad_clamp_fusion), kind=kCustom, calls=%fused_computation | custom fusion | bytes 186880 | tf_op jit(solution)/shard_map/jit(_take)/gather | solution.py:96
  58.5 2.3 %fusion.68 = bf16[640,2,4,9]{3,2,1,0:T(4,128)(2,1)S(1)} fusion(bf16[640,9,4,2]{1,2,3,0:T(4,128)(2,1)S(1)} %gather_fusion, pred[640]{0:T(1024)(128)(4,1)S(1)} %compare_and_fusion), kind=kLoop, calls=%fused_computation.150 | loop fusion | flops 46080 | bytes 184960
  60.9 2.1 %reshape.369 = bf16[32,2,720]{2,1,0:T(2,128)(2,1)} reshape(bf16[640,2,4,9]{3,2,1,0:T(4,128)(2,1)S(1)} %fusion.68) | data formatting | bytes 184320
  63.0 14.4 %all-to-all-start.1 = ((bf16[32,2,720]{2,1,0:T(2,128)(2,1)}), bf16[32,2,720]{2,1,0:T(2,128)(2,1)S(1)}, u32[]{:S(2)}, u32[]{:S(2)}) async-start(bf16[32,2,720]{2,1,0:T(2,128)(2,1)} %reshape.369), calls=%async_computation.1 | async-start | bytes 196608 | tf_op jit(solution)/shard_map/all_to_all | solution.py:104
  77.3 0.1 iota_compare_fusion
  77.4 9.6 %all-to-all-done.1 = bf16[32,2,720]{2,1,0:T(2,128)(2,1)S(1)} async-done(((bf16[32,2,720]{2,1,0:T(2,128)(2,1)}), bf16[32,2,720]{2,1,0:T(2,128)(2,1)S(1)}, u32[]{:S(2)}, u32[]{:S(2)}) %all-to-all-start.1) | async-done | bytes 92192 | tf_op jit(solution)/shard_map/all_to_all | solution.py:104
  87.0 1.6 %reshape.370 = bf16[640,2,4,9]{3,2,1,0:T(4,128)(2,1)S(1)} reshape(bf16[32,2,720]{2,1,0:T(2,128)(2,1)S(1)} %all-to-all-done.1) | data formatting | bytes 184320
  88.6 2.7 %copy.74 = bf16[9,4,2,32,20]{4,3,2,1,0:T(8,128)(2,1)S(1)} copy(bf16[9,4,2,32,20]{0,1,2,4,3:T(4,128)(2,1)S(1)} %bitcast.167) | data formatting | bytes 184320 | tf_op jit(solution)/shard_map/all_to_all | solution.py:104
  91.3 0.5 copy.62
  91.7 0.5 copy.63
  92.2 2.6 %fusion.9 = bf16[20,9,2,640]{3,1,2,0:T(8,128)(2,1)S(1)} fusion(bf16[9,128,2,20]{1,0,2,3:T(8,128)(2,1)S(1)} %copy.63, bf16[20,128,640]{2,1,0:T(8,128)(2,1)} %param.11, pred[20,640]{1,0:T(8,128)(4,1)S(1)} %iota_compare_fusion), kind=kOutput, calls=%fused_computation.17 | convolution fusion | flops 60851200 | bytes 3842560 | tf_op jit(solution)/shard_map/clts,sln->sctn/dot_general | solution.py:102
  94.8 1.1 %copy.64 = bf16[20,9,2,640]{3,2,1,0:T(2,128)(2,1)} copy(bf16[20,9,2,640]{3,1,2,0:T(8,128)(2,1)S(1)} %fusion.9) | data formatting | bytes 921600 | tf_op jit(solution)/shard_map/convert_element_type | solution.py:108
  (13 shorter events, 0.1 us)
Async XLA Ops:
  0.0 17.2 %copy-start.4 = (s32[4]{0:T(128)S(1)}, s32[4]{0:T(128)}, u32[]{:S(2)}) copy-start(s32[4]{0:T(128)} %param.9) | copy-start | bytes 52
  0.0 17.4 %copy-start.3 = (s32[640]{0:T(1024)S(1)}, s32[640]{0:T(1024)}, u32[]{:S(2)}) copy-start(s32[640]{0:T(1024)} %param.10) | copy-start | bytes 7684
  0.0 17.5 %copy-start.1 = (f32[4,4,321]{2,1,0:T(4,128)S(1)}, f32[4,4,321]{2,1,0:T(4,128)}, u32[]{:S(2)}) copy-start(f32[4,4,321]{2,1,0:T(4,128)} %param.7) | copy-start | bytes 61636
  0.0 17.5 %copy-start.2 = (s32[4,321]{1,0:T(4,128)S(1)}, s32[4,321]{1,0:T(4,128)}, u32[]{:S(2)}) copy-start(s32[4,321]{1,0:T(4,128)} %param.8) | copy-start | bytes 15412
  2.4 18.1 %collective-permute-start = (bf16[144,3,321]{2,1,0:T(4,128)(2,1)}, bf16[144,3,321]{2,1,0:T(4,128)(2,1)}, u32[]{:S(2)}, u32[]{:S(2)}) collective-permute-start(bf16[144,3,321]{2,1,0:T(4,128)(2,1)} %get-tuple-element.9), channel_id=1, source_target_pairs={{0,16},{16,32},{32,48},{48,64},{64,80},{80,96},{96,112},{112,128},... | collective-permute-start | bytes 832040 | tf_op jit(solution)/shard_map/ppermute | solution.py:19
  7.1 13.4 %collective-permute-start.1 = (bf16[144,3,321]{2,1,0:T(4,128)(2,1)S(1)}, bf16[144,3,321]{2,1,0:T(4,128)(2,1)}, u32[]{:S(2)}, u32[]{:S(2)}) collective-permute-start(bf16[144,3,321]{2,1,0:T(4,128)(2,1)S(1)} %get-tuple-element.10), channel_id=1, source_target_pairs={{16,0},{32,16},{48,32},{64,48},{80,64},{96,80},{112,96},{128,112},... | collective-permute-start | bytes 832040 | tf_op jit(solution)/shard_map/ppermute | solution.py:22
  17.6 2.9 %copy-start = (bf16[144,4,321]{2,1,0:T(4,128)(2,1)S(1)}, bf16[144,4,321]{2,1,0:T(4,128)(2,1)}, u32[]{:S(2)}) copy-start(bf16[144,4,321]{2,1,0:T(4,128)(2,1)} %param.6) | copy-start | bytes 1109380
  26.4 23.8 %all-to-all-start = ((bf16[16,9,4,321]{3,2,1,0:T(4,128)(2,1)}), bf16[16,9,4,321]{3,2,1,0:T(4,128)(2,1)S(1)}, u32[]{:S(2)}, u32[]{:S(2)}) async-start(bf16[16,9,4,321]{3,2,1,0:T(4,128)(2,1)} %bitcast.8), calls=%async_computation | async-start | bytes 884736 | tf_op jit(solution)/shard_map/all_to_all | solution.py:73
  63.0 24.0 %all-to-all-start.1 = ((bf16[32,2,720]{2,1,0:T(2,128)(2,1)}), bf16[32,2,720]{2,1,0:T(2,128)(2,1)S(1)}, u32[]{:S(2)}, u32[]{:S(2)}) async-start(bf16[32,2,720]{2,1,0:T(2,128)(2,1)} %reshape.369), calls=%async_computation.1 | async-start | bytes 196608 | tf_op jit(solution)/shard_map/all_to_all | solution.py:104

commit v2 on v1

--- a/solution.py
+++ b/solution.py
@@ -9,6 +9,7 @@
 NDEG = 640
 HALO = 3
 SPLIT = 64
+LAT = ("lat_outer", "lat_inner")
 
 
 def extended(block, sides, width):
@@ -54,9 +55,9 @@
     pieces = lax.axis_size("lon")
     keep = columns // pieces
     slots = legendre.shape[0]
-    first_row = lax.axis_index("lat") * band_rows
+    first_row = lax.axis_index(LAT) * band_rows
     first_point = lax.axis_index("lon") * seg_len
-    padded = extended(grid, (("lat", 1),), HALO)
+    padded = extended(grid, ((LAT, 1),), HALO)
     offset = dep_base - (first_row + jnp.arange(band_rows, dtype=jnp.int32))[:, None]
     arrival = jnp.zeros((columns, band_rows, seg_len), jnp.float32)
     for displace in range(-HALO, HALO + 1):
@@ -85,41 +86,59 @@
     imag_part = jnp.sum(
         phase_re[:, :, None, :] * spectra[:, 1] + phase_im[:, :, None, :] * spectra[:, 0], axis=1
     )
-    fourier = jnp.stack([real_part, imag_part], axis=2).transpose(1, 0, 2, 3)
+    fourier = jnp.stack([real_part, imag_part], axis=2)
     wavenumber = jnp.arange(M, dtype=jnp.int32)
     inverse = jnp.float32(1.0) / row_points.astype(jnp.float32)
     resolved = 2 * wavenumber[None, :] < row_points[:, None]
     fourier = jnp.where(
-        resolved[None, :, None, :], fourier * inverse[None, :, None, None], jnp.float32(0.0)
+        resolved[:, None, None, :], fourier * inverse[:, None, None, None], jnp.float32(0.0)
     )
     fourier = fourier.astype(jnp.bfloat16)
-    sorted_waves = jnp.take(fourier, wave_order, axis=3)
-    my_slots = lax.dynamic_slice_in_dim(wave_order, lax.axis_index("lat") * slots, slots)
+    pick = (wave_order[None, :] == wavenumber[:, None]).astype(jnp.bfloat16)
+    sorted_waves = jnp.einsum(
+        "rctm,ms->sctr", fourier, pick, preferred_element_type=jnp.float32
+    ).astype(jnp.bfloat16)
+    outer, inner = lax.axis_size(LAT[0]), lax.axis_size(LAT[1])
+    sorted_waves = sorted_waves.reshape((outer, inner, slots) + sorted_waves.shape[1:])
+    sorted_waves = lax.all_to_all(sorted_waves, LAT[1], split_axis=1, concat_axis=1, tiled=True)
+    sorted_waves = lax.all_to_all(sorted_waves, LAT[0], split_axis=0, concat_axis=0, tiled=True)
+    sorted_waves = sorted_waves.reshape((outer * inner,) + sorted_waves.shape[2:])
+    my_slots = lax.dynamic_slice_in_dim(wave_order, lax.axis_index(LAT) * slots, slots)
     degree = jnp.arange(NDEG, dtype=jnp.int32)
     masked_table = jnp.where(
         degree[None, None, :] >= my_slots[:, None, None], legendre, jnp.zeros((), legendre.dtype)
     )
+    masked_table = masked_table.reshape(slots, outer * inner, band_rows, NDEG)
     result = jnp.einsum(
-        "clts,sln->sctn",
-        lax.all_to_all(sorted_waves, "lat", split_axis=3, concat_axis=1, tiled=True),
-        masked_table,
-        preferred_element_type=jnp.float32,
+        "qsctr,sqrn->sctn", sorted_waves, masked_table, preferred_element_type=jnp.float32
     )
     return result.astype(jnp.bfloat16)
 
 
+def lat_split(mesh):
+    count = mesh.shape["lat"]
+    fast = len({tuple(getattr(d, "coords", (0,)))[0] for d in mesh.devices[:, 0]})
+    if fast < 1 or count % fast != 0:
+        fast = 1
+    return count // fast, fast
+
+
 def solution(mesh):
+    outer, inner = lat_split(mesh)
+    grid_mesh = jax.sharding.Mesh(
+        mesh.devices.reshape(outer, inner, mesh.shape["lon"]), LAT + ("lon",)
+    )
     return jax.shard_map(
         shards,
-        mesh=mesh,
+        mesh=grid_mesh,
         in_specs=(
-            P(None, "lat", "lon"),
-            P(None, "lat", "lon"),
-            P("lat", "lon"),
-            P("lat"),
+            P(None, LAT, "lon"),
+            P(None, LAT, "lon"),
+            P(LAT, "lon"),
+            P(LAT),
             P(),
-            P("lat", None, None),
+            P(LAT, None, None),
         ),
-        out_specs=P("lat", "lon", None, None),
+        out_specs=P(LAT, "lon", None, None),
         check_vma=False,
     )

time: 96.4 us -> 97.3 us (level)
  waiting for transfers between devices: 16.5 us -> 13.8 us
  starting transfers between devices: 28.6 us -> 30.8 us
  other arithmetic: 23.6 us -> 24.7 us
    reshape x0 -> x4, local copies, waits for them, and re-layouts: none -> 5.85 us  [the longest x1 3 us: shards(): masked_table = masked_table.reshape(slots, outer * inner, band_rows, NDEG)]
    gather x1 -> x0, local copies, waits for them, and re-layouts: 3.54 us -> none  [shards(): sorted_waves = jnp.take(fourier, wave_order, axis=3)]
    all_to_all x3 -> x2, local copies, waits for them, and re-layouts: 3.57 us -> 0.73 us  [the longest x1 0.46 us: shards(): lax.all_to_all(sorted_waves, LAT[1], split_axis=1, concat_axis=1, tiled=T...]
    all_to_all x1 -> x2, waiting for transfers between devices: 9.59 us -> 7.11 us  [the longest x1 4.98 us: shards(): lax.all_to_all(sorted_waves, LAT[1], split_axis=1, concat_axis=1, tiled=T...]
    unnamed x1 -> x0, other arithmetic: 2.34 us -> none
    select_n x1, other arithmetic: 0.01 us -> 2.28 us  [shards(): jnp.where(degree[None, None, :] >= my_slots[:, None, None], legendre, jnp...]
    all_to_all x1 -> x2, starting transfers between devices: 14.4 us -> 16.6 us  [the longest x1 11.6 us: shards(): lax.all_to_all(sorted_waves, LAT[0], split_axis=0, concat_axis=0, tiled=T...]
    unnamed x12 -> x14, local copies, waits for them, and re-layouts: 3.74 us -> 5.41 us
  transfers between devices with their start and end apart: 4 -> 5, of which waited for: 2 -> 3; matrix products, arithmetic and copies ran while one was open for 22% -> 28% of each run, Pallas kernels for 0% -> 0%
where the time goes in v2:
time: 97.3 us; the launch traced here: 96.6 us
  starting transfers between devices  30.8 us (32%)
  other arithmetic  24.7 us (25%)
  local copies, waits for them, and re-layouts  20.9 us (21%)
  waiting for transfers between devices  13.8 us (14%)
  matrix products  6.15 us (6%)
    all_to_all x1, starting transfers between devices, shards(): lax.all_to_all(sorted_waves, LAT[0], split_axis=0, concat_axis=0, tiled=T...  11.6 us
    all_to_all x1, starting transfers between devices, shards(): lax.all_to_all(arrival.reshape(pieces, keep, band_rows, seg_len), 'lon',...  8.07 us
    all_to_all x1, waiting for transfers between devices, shards(): lax.all_to_all(arrival.reshape(pieces, keep, band_rows, seg_len), 'lon',...  6.65 us
    convert_element_type x1, other arithmetic, shards(): jnp.where(inside[None], arrival, jnp.float32(0.0)).astype(jnp.bfloat16)  5.9 us
    unnamed x14, local copies, waits for them, and re-layouts  5.41 us
    cos x1, other arithmetic, segment_tables(): cl, sl = (jnp.cos(low)[..., None, :], jnp.sin(low)[..., None, :])  5.2 us
    all_to_all x1, waiting for transfers between devices, shards(): lax.all_to_all(sorted_waves, LAT[1], split_axis=1, concat_axis=1, tiled=T...  4.98 us
    all_to_all x1, starting transfers between devices, shards(): lax.all_to_all(sorted_waves, LAT[1], split_axis=1, concat_axis=1, tiled=T...  4.97 us
  transfers between devices with their start and end apart: 5, of which 3 were waited for; matrix products, arithmetic and copies ran while one was open for 28% of the time, Pallas kernels for 0%

profile of v2, /device:TPU:1, one launch (start us, length us, event | category | flops | bytes accessed | tf_op | source)
XLA Modules:
  0.0 96.6 jit_solution(8094316916858111340)
XLA Ops:
  0.0 1.5 %fusion.77 = (bf16[144,3,321]{2,1,0:T(4,128)(2,1)S(1)}, bf16[144,3,321]{2,1,0:T(4,128)(2,1)S(1)}) fusion(bf16[144,4,321]{2,1,0:T(4,128)(2,1)} %param.6), kind=kLoop, calls=%fused_computation.151 | loop fusion | bytes 1109376 | tf_op jit(solution)/shard_map/slice | solution.py:21
  1.5 0.0 copy-start.1
  1.5 0.0 copy-start.2
  1.6 0.0 copy-start
  1.6 4.9 %collective-permute-start = (bf16[144,3,321]{2,1,0:T(4,128)(2,1)S(1)}, bf16[144,3,321]{2,1,0:T(4,128)(2,1)}, u32[]{:S(2)}, u32[]{:S(2)}) collective-permute-start(bf16[144,3,321]{2,1,0:T(4,128)(2,1)S(1)} %get-tuple-element.9), channel_id=1, source_target_pairs={{0,16},{16,32},{32,48},{48,64},{64,80},{80,96},{96,112},{112,128},... | collective-permute-start | bytes 832040 | tf_op jit(solution)/shard_map/ppermute | solution.py:20
  6.4 1.3 %collective-permute-start.1 = (bf16[144,3,321]{2,1,0:T(4,128)(2,1)S(1)}, bf16[144,3,321]{2,1,0:T(4,128)(2,1)}, u32[]{:S(2)}, u32[]{:S(2)}) collective-permute-start(bf16[144,3,321]{2,1,0:T(4,128)(2,1)S(1)} %get-tuple-element.10), channel_id=1, source_target_pairs={{16,0},{32,16},{48,32},{64,48},{80,64},{96,80},{112,96},{128,112},... | collective-permute-start | bytes 832040 | tf_op jit(solution)/shard_map/ppermute | solution.py:23
  7.7 0.7 broadcast_compare_fusion.2
  8.4 0.7 broadcast_divide_fusion
  9.0 0.7 compare_select_fusion
  9.8 0.7 broadcast_compare_fusion.1
  10.6 0.1 iota_multiply_fusion.1
  10.6 1.4 %fusion.50 = (f32[4,321,10]{1,2,0:T(8,128)S(1)}, f32[4,321,10]{1,2,0:T(8,128)S(1)}) fusion(f32[4]{0:T(128)S(1)} %get-tuple-element.25, pred[4]{0:T(512)(128)(4,1)S(1)} %broadcast_compare_fusion.2, s32[4]{0:T(128)S(1)} %get-tuple-element.24, s32[321,10]{0,1:T(8,128)S(1)} %iota_multiply_fusion.1), kind=kLoop, calls=%fused_computation.77 | loop fusion | flops 128400 | bytes 115596 | tf_op jit(solution)/shard_map/cos | solution.py:37
  12.0 5.2 %fusion.31 = (f32[4,321,64]{1,2,0:T(8,128)S(1)}, f32[4,321,64]{1,2,0:T(8,128)S(1)}) fusion(f32[4]{0:T(128)S(1)} %get-tuple-element.25, pred[4]{0:T(512)(128)(4,1)S(1)} %broadcast_compare_fusion.2, s32[4]{0:T(128)S(1)} %get-tuple-element.24, s32[321,64]{0,1:T(8,128)S(1)} %iota_multiply_fusion), kind=kLoop, calls=%fused_computation.55 | loop fusion | flops 821760 | bytes 739620 | tf_op jit(solution)/shard_map/cos | solution.py:38
  17.2 0.8 fusion.55
  18.1 2.7 %subtract_convert_fusion = (bf16[4,321,10,64]{1,3,2,0:T(8,128)(2,1)}, bf16[4,321,10,64]{1,3,2,0:T(8,128)(2,1)S(1)}) fusion(f32[4,321,64]{1,2,0:T(8,128)S(1)} %get-tuple-element.12, f32[4,321,10]{1,2,0:T(8,128)S(1)} %get-tuple-element.21, f32[4,321,64]{1,2,0:T(8,128)S(1)} %get-tuple-element.11, f32[4,321,10]{1,2,0:T(8,128)S(1)} %get-tuple-element.20), kind=kLoop, calls=%fused_computation.1 | loop fusion | flops 7395840 | bytes 4047168 | tf_op jit(solution)/shard_map/convert.3
  20.8 0.1 fusion.51
  21.0 5.9 %select_convert_fusion = bf16[144,4,321]{2,1,0:T(4,128)(2,1)} fusion(bf16[144,4,321]{2,1,0:T(4,128)(2,1)S(1)} %copy-done, bf16[144,3,321]{2,1,0:T(4,128)(2,1)} %collective-permute-done.1, bf16[144,3,321]{2,1,0:T(4,128)(2,1)} %collective-permute-done, f32[4,321]{1,0:T(4,128)S(1)} %get-tuple-element.19, f32[4,321]{1,0:T(4,128)S(1)} %get-tuple-element.18, ...), kind=kLoop, calls=%fused_computation.32 | loop fusion | flops 7395840 | bytes 1331508 | tf_op jit(solution)/shard_map/convert_element_type | solution.py:73
  26.9 8.1 %all-to-all-start = ((bf16[16,9,4,321]{3,2,1,0:T(4,128)(2,1)}), bf16[16,9,4,321]{3,2,1,0:T(4,128)(2,1)S(1)}, u32[]{:S(2)}, u32[]{:S(2)}) async-start(bf16[16,9,4,321]{3,2,1,0:T(4,128)(2,1)} %bitcast.10), calls=%async_computation | async-start | bytes 884736 | tf_op jit(solution)/shard_map/all_to_all | solution.py:74
  34.9 0.0 copy-start.4
  34.9 0.0 copy-start.3
  35.0 3.9 %copy.31 = bf16[4,321,1,640]{3,1,2,0:T(8,128)(2,1)} copy(bf16[4,321,1,640]{1,3,0,2:T(8,128)(2,1)} %bitcast.173) | data formatting | bytes 3287040 | tf_op jit(solution)/shard_map/sub | solution.py:40
  38.8 2.3 %copy.32 = bf16[4,321,1,640]{3,1,2,0:T(8,128)(2,1)} copy(bf16[4,321,1,640]{1,3,0,2:T(8,128)(2,1)S(1)} %bitcast.172) | data formatting | bytes 3287040 | tf_op jit(solution)/shard_map/neg | solution.py:42
  41.2 0.1 dynamic_slice.3
  41.2 0.2 remainder_select_fusion.2
  41.4 0.1 broadcast_compare_fusion
  41.5 2.3 %fusion.48 = (f32[4,16,640]{2,1,0:T(8,128)S(1)}, f32[4,16,640]{2,1,0:T(8,128)S(1)}) fusion(f32[4]{0:T(128)S(1)} %get-tuple-element.25, pred[4]{0:T(512)(128)(4,1)S(1)} %broadcast_compare_fusion.2, s32[4]{0:T(128)S(1)} %get-tuple-element.24, s32[4,16]{1,0:T(4,128)S(1)} %remainder_select_fusion.2), kind=kLoop, calls=%fused_computation.74 | loop fusion | flops 491520 | bytes 327972 | tf_op jit(solution)/shard_map/cos | solution.py:50
  43.8 6.7 %all-to-all-done = bf16[16,9,4,321]{3,2,1,0:T(4,128)(2,1)S(1)} async-done(((bf16[16,9,4,321]{3,2,1,0:T(4,128)(2,1)}), bf16[16,9,4,321]{3,2,1,0:T(4,128)(2,1)S(1)}, u32[]{:S(2)}, u32[]{:S(2)}) %all-to-all-start) | async-done | bytes 369824 | tf_op jit(solution)/shard_map/all_to_all | solution.py:74
  50.4 2.9 %fusion.5 = f32[4,2,16,9,640]{4,2,3,1,0:T(8,128)S(1)} fusion(bf16[4,321,1,640]{3,1,2,0:T(8,128)(2,1)} %copy.32, bf16[4,321,1,640]{3,1,2,0:T(8,128)(2,1)} %copy.31, bf16[16,9,4,321,1]{3,2,1,0,4:T(4,128)(2,1)S(1)} %bitcast.180), kind=kOutput, calls=%fused_computation.9 | convolution fusion | flops 479907840 | bytes 6605952 | tf_op jit(solution)/shard_map/pcrj,rjtx->rtpcx/dot_general | solution.py:80
  53.3 0.7 subtract_reduce_fusion
  54.1 0.4 fusion.14
  54.5 1.4 %reshape.367 = bf16[8,4,20,9,2,4]{2,1,0,3,4,5:T(4,128)(2,1)S(1)} reshape(bf16[640,9,2,4]{0,1,2,3:T(8,128)(2,1)S(1)} %fusion.14) | data formatting | bytes 184320 | tf_op jit(solution)/shard_map/reshape | solution.py:102
  56.0 0.1 copy.62
  56.1 1.8 %reshape.368 = bf16[4,2,5760]{2,1,0:T(2,128)(2,1)} reshape(bf16[4,9,2,4,8,20]{5,4,3,2,1,0:T(8,128)(2,1)S(1)} %bitcast.175) | data formatting | bytes 184320
  57.9 5.0 %all-to-all-start.1 = ((bf16[4,2,5760]{2,1,0:T(2,128)(2,1)}), bf16[4,2,5760]{2,1,0:T(2,128)(2,1)S(1)}, u32[]{:S(2)}, u32[]{:S(2)}) async-start(bf16[4,2,5760]{2,1,0:T(2,128)(2,1)} %reshape.368), calls=%async_computation.1 | async-start | bytes 184320 | tf_op jit(solution)/shard_map/all_to_all | solution.py:103
  62.8 0.1 iota_compare_fusion.1
  62.9 5.0 %all-to-all-done.1 = bf16[4,2,5760]{2,1,0:T(2,128)(2,1)S(1)} async-done(((bf16[4,2,5760]{2,1,0:T(2,128)(2,1)}), bf16[4,2,5760]{2,1,0:T(2,128)(2,1)S(1)}, u32[]{:S(2)}, u32[]{:S(2)}) %all-to-all-start.1) | async-done | bytes 92192 | tf_op jit(solution)/shard_map/all_to_all | solution.py:103
  67.9 1.5 %reshape.369 = bf16[4,9,2,4,8,20]{5,4,3,2,1,0:T(8,128)(2,1)S(1)} reshape(bf16[4,2,5760]{2,1,0:T(2,128)(2,1)S(1)} %all-to-all-done.1) | data formatting | bytes 184320
  69.4 0.5 copy.63
  69.9 1.3 %reshape.370 = bf16[8,2,2880]{2,1,0:T(2,128)(2,1)} reshape(bf16[8,9,2,4,4,20]{5,4,3,2,1,0:T(4,128)(2,1)S(1)} %bitcast.177) | data formatting | bytes 184320
  71.2 11.6 %all-to-all-start.2 = ((bf16[8,2,2880]{2,1,0:T(2,128)(2,1)}), bf16[8,2,2880]{2,1,0:T(2,128)(2,1)S(1)}, u32[]{:S(2)}, u32[]{:S(2)}) async-start(bf16[8,2,2880]{2,1,0:T(2,128)(2,1)} %reshape.370), calls=%async_computation.2 | async-start | bytes 188416 | tf_op jit(solution)/shard_map/all_to_all | solution.py:104
  82.8 2.3 %broadcast_select_fusion = bf16[20,128,640]{2,1,0:T(8,128)(2,1)S(1)} fusion(bf16[20,128,640]{2,1,0:T(8,128)(2,1)} %param.11, pred[20,640]{1,0:T(8,128)(4,1)S(1)} %iota_compare_fusion.1), kind=kLoop, calls=%fused_computation.8 | loop fusion | flops 1638400 | bytes 6566400 | tf_op jit(solution)/shard_map/jit(_where)/select_n | solution.py:108
  85.1 3.0 %reshape.361 = bf16[20,32,4,640]{3,2,1,0:T(4,128)(2,1)} reshape(bf16[20,128,640]{2,1,0:T(8,128)(2,1)S(1)} %broadcast_select_fusion) | data formatting | bytes 6553600 | tf_op jit(solution)/shard_map/reshape | solution.py:111
  88.1 2.1 %all-to-all-done.2 = bf16[8,2,2880]{2,1,0:T(2,128)(2,1)S(1)} async-done(((bf16[8,2,2880]{2,1,0:T(2,128)(2,1)}), bf16[8,2,2880]{2,1,0:T(2,128)(2,1)S(1)}, u32[]{:S(2)}, u32[]{:S(2)}) %all-to-all-start.2) | async-done | bytes 92192 | tf_op jit(solution)/shard_map/all_to_all | solution.py:104
  90.2 0.8 reshape.371
  91.0 0.3 copy.38
  91.3 1.3 %copy.39 = bf16[32,20,9,2,4]{0,2,4,3,1:T(8,128)(2,1)S(1)} copy(bf16[32,20,9,2,4]{1,0,4,3,2:T(8,128)(2,1)S(1)} %bitcast.179) | data formatting | bytes 184320 | tf_op jit(solution)/shard_map/reshape | solution.py:105
  92.6 2.8 %bitcast_convert_fusion = bf16[20,9,2,640]{3,1,2,0:T(8,128)(2,1)S(1)} fusion(bf16[32,20,9,2,4]{0,2,4,3,1:T(8,128)(2,1)S(1)} %copy.39, bf16[20,32,4,640,1]{3,2,1,0,4:T(4,128)(2,1)} %bitcast.174), kind=kOutput, calls=%fused_computation.10 | convolution fusion | flops 59212800 | bytes 3829760 | tf_op jit(solution)/shard_map/qsctr,sqrn->sctn/dot_general | solution.py:112
  95.4 1.1 %copy.41 = bf16[20,9,2,640]{3,2,1,0:T(2,128)(2,1)} copy(bf16[20,9,2,640]{3,1,2,0:T(8,128)(2,1)S(1)} %bitcast_convert_fusion) | data formatting | bytes 921600 | tf_op jit(solution)/shard_map/convert_element_type | solution.py:115
  (13 shorter events, 0.0 us)
Async XLA Ops:
  1.5 19.3 %copy-start.1 = (f32[4,4,321]{2,1,0:T(4,128)S(1)}, f32[4,4,321]{2,1,0:T(4,128)}, u32[]{:S(2)}) copy-start(f32[4,4,321]{2,1,0:T(4,128)} %param.7) | copy-start | bytes 61636
  1.5 19.3 %copy-start.2 = (s32[4,321]{1,0:T(4,128)S(1)}, s32[4,321]{1,0:T(4,128)}, u32[]{:S(2)}) copy-start(s32[4,321]{1,0:T(4,128)} %param.8) | copy-start | bytes 15412
  1.6 19.4 %copy-start = (bf16[144,4,321]{2,1,0:T(4,128)(2,1)S(1)}, bf16[144,4,321]{2,1,0:T(4,128)(2,1)}, u32[]{:S(2)}) copy-start(bf16[144,4,321]{2,1,0:T(4,128)(2,1)} %param.6) | copy-start | bytes 1109380
  1.6 19.4 %collective-permute-start = (bf16[144,3,321]{2,1,0:T(4,128)(2,1)S(1)}, bf16[144,3,321]{2,1,0:T(4,128)(2,1)}, u32[]{:S(2)}, u32[]{:S(2)}) collective-permute-start(bf16[144,3,321]{2,1,0:T(4,128)(2,1)S(1)} %get-tuple-element.9), channel_id=1, source_target_pairs={{0,16},{16,32},{32,48},{48,64},{64,80},{80,96},{96,112},{112,128},... | collective-permute-start | bytes 832040 | tf_op jit(solution)/shard_map/ppermute | solution.py:20
  6.4 14.5 %collective-permute-start.1 = (bf16[144,3,321]{2,1,0:T(4,128)(2,1)S(1)}, bf16[144,3,321]{2,1,0:T(4,128)(2,1)}, u32[]{:S(2)}, u32[]{:S(2)}) collective-permute-start(bf16[144,3,321]{2,1,0:T(4,128)(2,1)S(1)} %get-tuple-element.10), channel_id=1, source_target_pairs={{16,0},{32,16},{48,32},{64,48},{80,64},{96,80},{112,96},{128,112},... | collective-permute-start | bytes 832040 | tf_op jit(solution)/shard_map/ppermute | solution.py:23
  26.9 23.6 %all-to-all-start = ((bf16[16,9,4,321]{3,2,1,0:T(4,128)(2,1)}), bf16[16,9,4,321]{3,2,1,0:T(4,128)(2,1)S(1)}, u32[]{:S(2)}, u32[]{:S(2)}) async-start(bf16[16,9,4,321]{3,2,1,0:T(4,128)(2,1)} %bitcast.10), calls=%async_computation | async-start | bytes 884736 | tf_op jit(solution)/shard_map/all_to_all | solution.py:74
  34.9 6.2 %copy-start.4 = (s32[640]{0:T(1024)S(1)}, s32[640]{0:T(1024)}, u32[]{:S(2)}) copy-start(s32[640]{0:T(1024)} %param.10) | copy-start | bytes 7684
  34.9 6.5 %copy-start.3 = (s32[4]{0:T(128)S(1)}, s32[4]{0:T(128)}, u32[]{:S(2)}) copy-start(s32[4]{0:T(128)} %param.9) | copy-start | bytes 52
  57.9 10.0 %all-to-all-start.1 = ((bf16[4,2,5760]{2,1,0:T(2,128)(2,1)}), bf16[4,2,5760]{2,1,0:T(2,128)(2,1)S(1)}, u32[]{:S(2)}, u32[]{:S(2)}) async-start(bf16[4,2,5760]{2,1,0:T(2,128)(2,1)} %reshape.368), calls=%async_computation.1 | async-start | bytes 184320 | tf_op jit(solution)/shard_map/all_to_all | solution.py:103
  71.2 19.0 %all-to-all-start.2 = ((bf16[8,2,2880]{2,1,0:T(2,128)(2,1)}), bf16[8,2,2880]{2,1,0:T(2,128)(2,1)S(1)}, u32[]{:S(2)}, u32[]{:S(2)}) async-start(bf16[8,2,2880]{2,1,0:T(2,128)(2,1)} %reshape.370), calls=%async_computation.2 | async-start | bytes 188416 | tf_op jit(solution)/shard_map/all_to_all | solution.py:104

commit v3 on v2

--- a/solution.py
+++ b/solution.py
@@ -8,7 +8,7 @@
 M = 640
 NDEG = 640
 HALO = 3
-SPLIT = 64
+SPLIT = 32
 LAT = ("lat_outer", "lat_inner")
 
 
@@ -31,15 +31,15 @@
 
 
 def segment_tables(points, seg_len, waves):
-    position = jnp.arange(seg_len, dtype=jnp.int32)
-    high = angles_of(points, position, jnp.arange(waves // SPLIT, dtype=jnp.int32) * SPLIT)
-    low = angles_of(points, position, jnp.arange(SPLIT, dtype=jnp.int32))
-    ch, sh = jnp.cos(high)[..., :, None], jnp.sin(high)[..., :, None]
-    cl, sl = jnp.cos(low)[..., None, :], jnp.sin(low)[..., None, :]
-    shape = (points.shape[0], seg_len, waves)
-    cosine = (ch * cl - sh * sl).reshape(shape)
-    sine = (sh * cl + ch * sl).reshape(shape)
-    return jnp.stack([cosine, -sine], axis=2).astype(jnp.bfloat16)
+    wavenumber = jnp.arange(waves, dtype=jnp.int32)
+    high = angles_of(points, jnp.arange(-(-seg_len // SPLIT), dtype=jnp.int32) * SPLIT, wavenumber)
+    low = angles_of(points, jnp.arange(SPLIT, dtype=jnp.int32), wavenumber)
+    ch, sh = jnp.cos(high)[:, :, None, :], jnp.sin(high)[:, :, None, :]
+    cl, sl = jnp.cos(low)[:, None, :, :], jnp.sin(low)[:, None, :, :]
+    cosine = ch * cl - sh * sl
+    sine = sh * cl + ch * sl
+    table = jnp.concatenate([cosine, -sine], axis=3).astype(jnp.bfloat16)
+    return table.reshape(points.shape[0], -1, 2 * waves)[:, :seg_len]
 
 
 def phase_pair(points, starts, waves):
@@ -78,13 +78,14 @@
     starts = jnp.arange(pieces, dtype=jnp.int32) * seg_len
     phase_re, phase_im = phase_pair(row_points, starts, M)
     spectra = jnp.einsum(
-        "pcrj,rjtx->rtpcx", gathered, tables, preferred_element_type=jnp.float32
-    )
+        "pcrj,rjx->rpcx", gathered, tables, preferred_element_type=jnp.float32
+    ).reshape(band_rows, pieces, keep, 2, M)
+    spectra_re, spectra_im = spectra[:, :, :, 0], spectra[:, :, :, 1]
     real_part = jnp.sum(
-        phase_re[:, :, None, :] * spectra[:, 0] - phase_im[:, :, None, :] * spectra[:, 1], axis=1
+        phase_re[:, :, None, :] * spectra_re - phase_im[:, :, None, :] * spectra_im, axis=1
     )
     imag_part = jnp.sum(
-        phase_re[:, :, None, :] * spectra[:, 1] + phase_im[:, :, None, :] * spectra[:, 0], axis=1
+        phase_re[:, :, None, :] * spectra_im + phase_im[:, :, None, :] * spectra_re, axis=1
     )
     fourier = jnp.stack([real_part, imag_part], axis=2)
     wavenumber = jnp.arange(M, dtype=jnp.int32)
@@ -98,19 +99,16 @@
     sorted_waves = jnp.einsum(
         "rctm,ms->sctr", fourier, pick, preferred_element_type=jnp.float32
     ).astype(jnp.bfloat16)
-    outer, inner = lax.axis_size(LAT[0]), lax.axis_size(LAT[1])
-    sorted_waves = sorted_waves.reshape((outer, inner, slots) + sorted_waves.shape[1:])
-    sorted_waves = lax.all_to_all(sorted_waves, LAT[1], split_axis=1, concat_axis=1, tiled=True)
-    sorted_waves = lax.all_to_all(sorted_waves, LAT[0], split_axis=0, concat_axis=0, tiled=True)
-    sorted_waves = sorted_waves.reshape((outer * inner,) + sorted_waves.shape[2:])
+    count = lax.axis_size(LAT)
+    sorted_waves = sorted_waves.reshape((count, slots) + sorted_waves.shape[1:])
+    sorted_waves = lax.all_to_all(sorted_waves, LAT, split_axis=0, concat_axis=4, tiled=True)[0]
     my_slots = lax.dynamic_slice_in_dim(wave_order, lax.axis_index(LAT) * slots, slots)
     degree = jnp.arange(NDEG, dtype=jnp.int32)
     masked_table = jnp.where(
         degree[None, None, :] >= my_slots[:, None, None], legendre, jnp.zeros((), legendre.dtype)
     )
-    masked_table = masked_table.reshape(slots, outer * inner, band_rows, NDEG)
     result = jnp.einsum(
-        "qsctr,sqrn->sctn", sorted_waves, masked_table, preferred_element_type=jnp.float32
+        "sctl,sln->sctn", sorted_waves, masked_table, preferred_element_type=jnp.float32
     )
     return result.astype(jnp.bfloat16)
 

time: 97.3 us -> 93.6 us (0.962)
  waiting for transfers between devices: 13.8 us -> 17.8 us
  local copies, waits for them, and re-layouts: 20.9 us -> 17.1 us
  starting transfers between devices: 30.8 us -> 28.2 us
    slice x0 -> x1, local copies, waits for them, and re-layouts: none -> 5.75 us  [shards(): spectra_re, spectra_im = (spectra[:, :, :, 0], spectra[:, :, :, 1])]
    sub x1 -> x0, local copies, waits for them, and re-layouts: 3.89 us -> none  [segment_tables(): cosine = (ch * cl - sh * sl).reshape(shape)]
    unnamed x14, local copies, waits for them, and re-layouts: 5.41 us -> 1.76 us
    all_to_all x2 -> x1, waiting for transfers between devices: 7.11 us -> 9.8 us  [shards(): lax.all_to_all(sorted_waves, LAT, split_axis=0, concat_axis=4, tiled=True)]
    neg x1 -> x0, local copies, waits for them, and re-layouts: 2.3 us -> none  [segment_tables(): return jnp.stack([cosine, -sine], axis=2).astype(jnp.bfloat16)]
    select_n x1 -> x0, other arithmetic: 2.28 us -> none  [shards(): jnp.where(degree[None, None, :] >= my_slots[:, None, None], legendre, jnp...]
    convert_element_type x1, other arithmetic: 5.9 us -> 3.66 us  [shards(): jnp.where(inside[None], arrival, jnp.float32(0.0)).astype(jnp.bfloat16)]
    all_to_all x2 -> x1, starting transfers between devices: 16.6 us -> 14.8 us  [shards(): lax.all_to_all(sorted_waves, LAT, split_axis=0, concat_axis=4, tiled=True)]
  transfers between devices with their start and end apart: 5 -> 4, of which waited for: 3 -> 2; matrix products, arithmetic and copies ran while one was open for 28% -> 22% of each run, Pallas kernels for 0% -> 0%
where the time goes in v3:
time: 93.6 us; the launch traced here: 93.1 us
  starting transfers between devices  28.2 us (30%)
  other arithmetic  23.8 us (25%)
  waiting for transfers between devices  17.8 us (19%)
  local copies, waits for them, and re-layouts  17.1 us (18%)
  matrix products  5.9 us (6%)
    all_to_all x1, starting transfers between devices, shards(): lax.all_to_all(sorted_waves, LAT, split_axis=0, concat_axis=4, tiled=True)  14.8 us
    all_to_all x1, waiting for transfers between devices, shards(): lax.all_to_all(sorted_waves, LAT, split_axis=0, concat_axis=4, tiled=True)  9.8 us
    all_to_all x1, starting transfers between devices, shards(): lax.all_to_all(arrival.reshape(pieces, keep, band_rows, seg_len), 'lon',...  8.07 us
    all_to_all x1, waiting for transfers between devices, shards(): lax.all_to_all(arrival.reshape(pieces, keep, band_rows, seg_len), 'lon',...  8.03 us
    slice x1, local copies, waits for them, and re-layouts, shards(): spectra_re, spectra_im = (spectra[:, :, :, 0], spectra[:, :, :, 1])  5.75 us
    cos x1, other arithmetic, segment_tables(): cl, sl = (jnp.cos(low)[:, None, :, :], jnp.sin(low)[:, None, :, :])  4.36 us
    ppermute x1, starting transfers between devices, extended(): lax.ppermute(lax.slice_in_dim(block, block.shape[dim] - width, None, axis...  3.96 us
    convert_element_type x1, other arithmetic, shards(): jnp.where(inside[None], arrival, jnp.float32(0.0)).astype(jnp.bfloat16)  3.66 us
  transfers between devices with their start and end apart: 4, of which 2 were waited for; matrix products, arithmetic and copies ran while one was open for 22% of the time, Pallas kernels for 0%

profile of v3, /device:TPU:1, one launch (start us, length us, event | category | flops | bytes accessed | tf_op | source)
XLA Modules:
  0.0 93.1 jit_solution(8979089760492932723)
XLA Ops:
  0.0 1.6 %fusion.87 = (bf16[144,3,321]{2,1,0:T(4,128)(2,1)S(1)}, bf16[144,3,321]{2,1,0:T(4,128)(2,1)S(1)}) fusion(bf16[144,4,321]{2,1,0:T(4,128)(2,1)} %param.6), kind=kLoop, calls=%fused_computation.157 | loop fusion | bytes 1109376 | tf_op jit(solution)/shard_map/slice | solution.py:21
  1.6 4.0 %collective-permute-start = (bf16[144,3,321]{2,1,0:T(4,128)(2,1)S(1)}, bf16[144,3,321]{2,1,0:T(4,128)(2,1)S(1)}, u32[]{:S(2)}, u32[]{:S(2)}) collective-permute-start(bf16[144,3,321]{2,1,0:T(4,128)(2,1)S(1)} %get-tuple-element.11), channel_id=1, source_target_pairs={{0,16},{16,32},{32,48},{48,64},{64,80},{80,96},{96,112},{112,128},... | collective-permute-start | bytes 832040 | tf_op jit(solution)/shard_map/ppermute | solution.py:20
  5.6 1.3 %collective-permute-start.1 = (bf16[144,3,321]{2,1,0:T(4,128)(2,1)S(1)}, bf16[144,3,321]{2,1,0:T(4,128)(2,1)S(1)}, u32[]{:S(2)}, u32[]{:S(2)}) collective-permute-start(bf16[144,3,321]{2,1,0:T(4,128)(2,1)S(1)} %get-tuple-element.12), channel_id=1, source_target_pairs={{16,0},{32,16},{48,32},{64,48},{80,64},{96,80},{112,96},{128,112},... | collective-permute-start | bytes 832040 | tf_op jit(solution)/shard_map/ppermute | solution.py:23
  6.9 0.9 fusion.59
  7.7 0.8 fusion.63
  8.6 0.7 compare_select_fusion
  9.3 0.7 broadcast_compare_fusion.2
  10.0 0.7 broadcast_compare_fusion.1
  10.7 0.1 iota_multiply_fusion.1
  10.8 1.3 %broadcast_compare_fusion = pred[4,640]{1,0:T(4,128)(4,1)} fusion(s32[640]{0:T(1024)S(1)} %iota_multiply_fusion.2, s32[4]{0:T(128)} %param.9), kind=kLoop, calls=%fused_computation.132 | loop fusion | flops 2560 | bytes 5136 | tf_op jit(solution)/shard_map/lt | solution.py:93
  12.1 0.2 remainder_select_fusion.2
  12.3 3.0 %fusion.58 = (f32[4,16,640]{2,1,0:T(8,128)S(1)}, f32[4,16,640]{2,1,0:T(8,128)}) fusion(f32[4]{0:T(128)S(1)} %get-tuple-element.27, pred[4]{0:T(512)(128)(4,1)S(1)} %broadcast_compare_fusion.2, s32[4]{0:T(128)S(1)} %get-tuple-element.26, s32[4,16]{1,0:T(4,128)S(1)} %remainder_select_fusion.2), kind=kLoop, calls=%fused_computation.80 | loop fusion | flops 491520 | bytes 327972 | tf_op jit(solution)/shard_map/cos | solution.py:50
  15.3 1.2 %broadcast_divide_fusion = f32[4]{0:T(128)} fusion(s32[4]{0:T(128)} %param.9), kind=kLoop, calls=%fused_computation.150 | loop fusion | flops 8 | bytes 32 | tf_op jit(solution)/shard_map/div | solution.py:92
  16.5 1.3 %dynamic_slice.3 = s32[20]{0:T(128)} dynamic-slice(s32[640]{0:T(1024)} %param.10, s32[]{:T(128)S(6)} %select_n.190), dynamic_slice_sizes={20} | dynamic-slice | bytes 164 | tf_op jit(solution)/shard_map/dynamic_slice | solution.py:105
  17.8 2.2 %fusion.57 = (f32[4,11,640]{2,1,0:T(8,128)S(1)}, f32[4,11,640]{2,1,0:T(8,128)S(1)}) fusion(f32[4]{0:T(128)S(1)} %get-tuple-element.27, pred[4]{0:T(512)(128)(4,1)S(1)} %broadcast_compare_fusion.2, s32[4]{0:T(128)S(1)} %get-tuple-element.26, s32[11,640]{1,0:T(8,128)S(1)} %iota_multiply_fusion.1), kind=kLoop, calls=%fused_computation.79 | loop fusion | flops 281600 | bytes 253476 | tf_op jit(solution)/shard_map/cos | solution.py:37
  20.1 0.0 collective-permute-done
  20.1 0.0 collective-permute-done.1
  20.1 0.0 copy-done
  20.1 3.7 %select_convert_fusion = bf16[144,4,321]{2,1,0:T(4,128)(2,1)} fusion(bf16[144,4,321]{2,1,0:T(4,128)(2,1)S(1)} %copy-done, bf16[144,3,321]{2,1,0:T(4,128)(2,1)S(1)} %collective-permute-done.1, bf16[144,3,321]{2,1,0:T(4,128)(2,1)S(1)} %collective-permute-done, f32[4,321]{1,0:T(4,128)S(1)} %get-tuple-element.23, f32[4,321]{1,0:T(4,128)S(1)} %get-tuple-element.22, ...), kind=kLoop, calls=%fused_computation.32 | loop fusion | flops 7395840 | bytes 1331508 | tf_op jit(solution)/shard_map/convert_element_type | solution.py:73
  23.7 8.1 %all-to-all-start = ((bf16[16,9,4,321]{3,2,1,0:T(4,128)(2,1)}), bf16[16,9,4,321]{3,2,1,0:T(4,128)(2,1)S(1)}, u32[]{:S(2)}, u32[]{:S(2)}) async-start(bf16[16,9,4,321]{3,2,1,0:T(4,128)(2,1)} %bitcast.6), calls=%async_computation | async-start | bytes 884736 | tf_op jit(solution)/shard_map/all_to_all | solution.py:74
  31.8 4.4 %fusion.50 = (f32[4,32,640]{2,1,0:T(8,128)S(1)}, f32[4,32,640]{2,1,0:T(8,128)S(1)}) fusion(f32[4]{0:T(128)S(1)} %get-tuple-element.27, pred[4]{0:T(512)(128)(4,1)S(1)} %broadcast_compare_fusion.2, s32[4]{0:T(128)S(1)} %get-tuple-element.26, s32[32,640]{1,0:T(8,128)S(1)} %iota_multiply_fusion), kind=kLoop, calls=%fused_computation.71 | loop fusion | flops 819200 | bytes 737316 | tf_op jit(solution)/shard_map/cos | solution.py:38
  36.2 3.1 %subtract_convert_fusion = (bf16[4,11,32,640]{3,2,1,0:T(8,128)(2,1)}, bf16[4,11,32,640]{3,2,1,0:T(8,128)(2,1)}) fusion(f32[4,32,640]{2,1,0:T(8,128)S(1)} %get-tuple-element.14, f32[4,11,640]{2,1,0:T(8,128)S(1)} %get-tuple-element.16, f32[4,32,640]{2,1,0:T(8,128)S(1)} %get-tuple-element.13, f32[4,11,640]{2,1,0:T(8,128)S(1)} %get-tuple-element.15), kind=kLoop, calls=%fused_computation.1 | loop fusion | flops 8110080 | bytes 4485120 | tf_op jit(solution)/shard_map/convert.3
  39.3 8.0 %all-to-all-done = bf16[16,9,4,321]{3,2,1,0:T(4,128)(2,1)S(1)} async-done(((bf16[16,9,4,321]{3,2,1,0:T(4,128)(2,1)}), bf16[16,9,4,321]{3,2,1,0:T(4,128)(2,1)S(1)}, u32[]{:S(2)}, u32[]{:S(2)}) %all-to-all-start) | async-done | bytes 369824 | tf_op jit(solution)/shard_map/all_to_all | solution.py:74
  47.3 2.9 %fusion.1 = f32[4,16,9,1280]{3,1,2,0:T(8,128)S(1)} fusion(bf16[4,352,640]{2,1,0:T(8,128)(2,1)} %bitcast.179, bf16[4,352,640]{2,1,0:T(8,128)(2,1)} %bitcast.178, bf16[16,9,4,321]{3,2,1,0:T(4,128)(2,1)S(1)} %all-to-all-done), kind=kOutput, calls=%fused_computation.4 | convolution fusion | flops 479907840 | bytes 6923392 | tf_op jit(solution)/shard_map/pcrj,rjx->rpcx/dot_general | solution.py:80
  50.2 2.7 %reshape.269 = f32[4,16,9,2,640]{4,3,1,2,0:T(2,128)} reshape(f32[4,16,9,1280]{3,1,2,0:T(8,128)S(1)} %fusion.1) | data formatting | bytes 5898240 | tf_op jit(solution)/shard_map/reshape | solution.py:82
  53.0 5.8 %fusion.86 = (f32[4,16,9,1,640]{4,3,1,2,0:T(1,128)S(1)}, f32[4,16,9,1,640]{4,3,1,2,0:T(1,128)S(1)}) fusion(f32[4,16,9,2,640]{4,3,1,2,0:T(2,128)} %reshape.269), kind=kLoop, calls=%fused_computation.156 | loop fusion | bytes 5898240 | tf_op jit(solution)/shard_map/slice | solution.py:83
  58.7 0.0 copy-start.2
  58.7 0.0 copy-start.4
  58.7 0.0 copy-start.5
  58.8 0.0 copy-done.1
  58.8 0.8 fusion.13
  59.5 0.0 copy-done.2
  59.5 0.0 copy-done.4
  59.5 0.0 copy-done.5
  59.6 0.4 fusion.22
  60.0 1.4 %reshape.274 = bf16[32,20,9,2,4]{1,0,2,3,4:T(8,128)(2,1)S(1)} reshape(bf16[640,9,2,4]{0,1,2,3:T(8,128)(2,1)S(1)} %fusion.22) | data formatting | bytes 184320 | tf_op jit(solution)/shard_map/reshape | solution.py:103
  61.5 0.5 copy.48
  61.9 1.4 %reshape.275 = bf16[32,2,720]{2,1,0:T(2,128)(2,1)} reshape(bf16[32,9,2,4,20]{4,3,2,1,0:T(4,128)(2,1)S(1)} %bitcast.180) | data formatting | bytes 184320
  63.3 14.8 %all-to-all-start.1 = ((bf16[32,2,720]{2,1,0:T(2,128)(2,1)}), bf16[32,2,720]{2,1,0:T(2,128)(2,1)S(1)}, u32[]{:S(2)}, u32[]{:S(2)}) async-start(bf16[32,2,720]{2,1,0:T(2,128)(2,1)} %reshape.275), calls=%async_computation.1 | async-start | bytes 196608 | tf_op jit(solution)/shard_map/all_to_all | solution.py:104
  78.1 0.0 copy-done.3
  78.2 0.1 iota_compare_fusion.1
  78.2 9.8 %all-to-all-done.1 = bf16[32,2,720]{2,1,0:T(2,128)(2,1)S(1)} async-done(((bf16[32,2,720]{2,1,0:T(2,128)(2,1)}), bf16[32,2,720]{2,1,0:T(2,128)(2,1)S(1)}, u32[]{:S(2)}, u32[]{:S(2)}) %all-to-all-start.1) | async-done | bytes 92192 | tf_op jit(solution)/shard_map/all_to_all | solution.py:104
  88.0 0.4 reshape.276
  88.4 0.2 bitcast_bitcast_fusion
  88.6 0.3 copy.28
  88.9 0.5 copy.29
  89.4 2.6 %fusion.16 = bf16[20,9,2,640]{3,1,2,0:T(8,128)(2,1)S(1)} fusion(bf16[20,9,2,128]{3,1,2,0:T(8,128)(2,1)S(1)} %copy.29, bf16[20,128,640]{2,1,0:T(8,128)(2,1)} %param.11, pred[20,640]{1,0:T(8,128)(4,1)S(1)} %iota_compare_fusion.1), kind=kOutput, calls=%fused_computation.21 | convolution fusion | flops 60851200 | bytes 3842560 | tf_op jit(solution)/shard_map/sctl,sln->sctn/dot_general | solution.py:110
  91.9 1.1 %copy.30 = bf16[20,9,2,640]{3,2,1,0:T(2,128)(2,1)} copy(bf16[20,9,2,640]{3,1,2,0:T(8,128)(2,1)S(1)} %fusion.16) | data formatting | bytes 921600 | tf_op jit(solution)/shard_map/convert_element_type | solution.py:113
  (9 shorter events, 0.0 us)
Async XLA Ops:
  0.0 20.1 %copy-start = (bf16[144,4,321]{2,1,0:T(4,128)(2,1)S(1)}, bf16[144,4,321]{2,1,0:T(4,128)(2,1)}, u32[]{:S(2)}) copy-start(bf16[144,4,321]{2,1,0:T(4,128)(2,1)} %param.6) | copy-start | bytes 1109380
  1.6 18.5 %collective-permute-start = (bf16[144,3,321]{2,1,0:T(4,128)(2,1)S(1)}, bf16[144,3,321]{2,1,0:T(4,128)(2,1)S(1)}, u32[]{:S(2)}, u32[]{:S(2)}) collective-permute-start(bf16[144,3,321]{2,1,0:T(4,128)(2,1)S(1)} %get-tuple-element.11), channel_id=1, source_target_pairs={{0,16},{16,32},{32,48},{48,64},{64,80},{80,96},{96,112},{112,128},... | collective-permute-start | bytes 832040 | tf_op jit(solution)/shard_map/ppermute | solution.py:20
  5.6 14.5 %collective-permute-start.1 = (bf16[144,3,321]{2,1,0:T(4,128)(2,1)S(1)}, bf16[144,3,321]{2,1,0:T(4,128)(2,1)S(1)}, u32[]{:S(2)}, u32[]{:S(2)}) collective-permute-start(bf16[144,3,321]{2,1,0:T(4,128)(2,1)S(1)} %get-tuple-element.12), channel_id=1, source_target_pairs={{16,0},{32,16},{48,32},{64,48},{80,64},{96,80},{112,96},{128,112},... | collective-permute-start | bytes 832040 | tf_op jit(solution)/shard_map/ppermute | solution.py:23
  23.7 23.6 %all-to-all-start = ((bf16[16,9,4,321]{3,2,1,0:T(4,128)(2,1)}), bf16[16,9,4,321]{3,2,1,0:T(4,128)(2,1)S(1)}, u32[]{:S(2)}, u32[]{:S(2)}) async-start(bf16[16,9,4,321]{3,2,1,0:T(4,128)(2,1)} %bitcast.6), calls=%async_computation | async-start | bytes 884736 | tf_op jit(solution)/shard_map/all_to_all | solution.py:74
  53.0 5.8 %copy-start.1 = (f32[4,16,640]{2,1,0:T(8,128)S(1)}, f32[4,16,640]{2,1,0:T(8,128)}, u32[]{:S(2)}) copy-start(f32[4,16,640]{2,1,0:T(8,128)} %get-tuple-element.25) | copy-start | bytes 491524
  58.7 0.8 copy-start.2
  58.7 0.8 copy-start.4
  58.7 0.8 copy-start.5
  59.6 18.6 %copy-start.3 = (s32[20]{0:T(128)S(1)}, s32[20]{0:T(128)}, u32[]{:S(2)}) copy-start(s32[20]{0:T(128)} %dynamic_slice.3) | copy-start | bytes 244
  63.3 24.7 %all-to-all-start.1 = ((bf16[32,2,720]{2,1,0:T(2,128)(2,1)}), bf16[32,2,720]{2,1,0:T(2,128)(2,1)S(1)}, u32[]{:S(2)}, u32[]{:S(2)}) async-start(bf16[32,2,720]{2,1,0:T(2,128)(2,1)} %reshape.275), calls=%async_computation.1 | async-start | bytes 196608 | tf_op jit(solution)/shard_map/all_to_all | solution.py:104

commit v4 on v3

--- a/solution.py
+++ b/solution.py
@@ -25,17 +25,32 @@
     return block
 
 
-def angles_of(points, position, wavenumber):
-    product = position[None, :, None] * wavenumber[None, None, :] % points[:, None, None]
-    return 2.0 * math.pi * product.astype(jnp.float32) / points[:, None, None].astype(jnp.float32)
+def turn_sincos(product, points):
+    n = points.astype(jnp.float32)
+    quarter = 4.0 * product.astype(jnp.float32)
+    turn = jnp.floor(quarter * (1.0 / n) + 0.5)
+    x = (quarter - turn * n) * (0.5 * math.pi / n)
+    x2 = x * x
+    sine = x * (1.0 + x2 * (-1.0 / 6 + x2 * (1.0 / 120 + x2 * (-1.0 / 5040 + x2 * (1.0 / 362880)))))
+    cosine = 1.0 + x2 * (-0.5 + x2 * (1.0 / 24 + x2 * (-1.0 / 720 + x2 * (1.0 / 40320 - x2 * (1.0 / 3628800)))))
+    quadrant = turn.astype(jnp.int32) & 3
+    swap = (quadrant & 1) == 1
+    cos_out = jnp.where(swap, sine, cosine)
+    sin_out = jnp.where(swap, cosine, sine)
+    cos_out = jnp.where((quadrant == 1) | (quadrant == 2), -cos_out, cos_out)
+    sin_out = jnp.where(quadrant >= 2, -sin_out, sin_out)
+    return cos_out, sin_out
 
 
 def segment_tables(points, seg_len, waves):
     wavenumber = jnp.arange(waves, dtype=jnp.int32)
-    high = angles_of(points, jnp.arange(-(-seg_len // SPLIT), dtype=jnp.int32) * SPLIT, wavenumber)
-    low = angles_of(points, jnp.arange(SPLIT, dtype=jnp.int32), wavenumber)
-    ch, sh = jnp.cos(high)[:, :, None, :], jnp.sin(high)[:, :, None, :]
-    cl, sl = jnp.cos(low)[:, None, :, :], jnp.sin(low)[:, None, :, :]
+    high = jnp.arange(-(-seg_len // SPLIT), dtype=jnp.int32) * SPLIT
+    low = jnp.arange(SPLIT, dtype=jnp.int32)
+    rows = points[:, None, None]
+    ch, sh = turn_sincos(high[None, :, None] * wavenumber[None, None, :], rows)
+    cl, sl = turn_sincos(low[None, :, None] * wavenumber[None, None, :], rows)
+    ch, sh = ch[:, :, None, :], sh[:, :, None, :]
+    cl, sl = cl[:, None, :, :], sl[:, None, :, :]
     cosine = ch * cl - sh * sl
     sine = sh * cl + ch * sl
     table = jnp.concatenate([cosine, -sine], axis=3).astype(jnp.bfloat16)
@@ -44,10 +59,8 @@
 
 def phase_pair(points, starts, waves):
     wavenumber = jnp.arange(waves, dtype=jnp.int32)
-    shifted = starts[None, :] % points[:, None]
-    product = shifted[:, :, None] * wavenumber[None, None, :] % points[:, None, None]
-    angles = 2.0 * math.pi * product.astype(jnp.float32) / points[:, None, None].astype(jnp.float32)
-    return (jnp.cos(angles), -jnp.sin(angles))
+    cosine, sine = turn_sincos(starts[None, :, None] * wavenumber[None, None, :], points[:, None, None])
+    return (cosine, -sine)
 
 
 def shards(grid, cubic_weights, dep_base, row_points, wave_order, legendre):
@@ -79,8 +92,8 @@
     phase_re, phase_im = phase_pair(row_points, starts, M)
     spectra = jnp.einsum(
         "pcrj,rjx->rpcx", gathered, tables, preferred_element_type=jnp.float32
-    ).reshape(band_rows, pieces, keep, 2, M)
-    spectra_re, spectra_im = spectra[:, :, :, 0], spectra[:, :, :, 1]
+    )
+    spectra_re, spectra_im = spectra[..., :M], spectra[..., M:]
     real_part = jnp.sum(
         phase_re[:, :, None, :] * spectra_re - phase_im[:, :, None, :] * spectra_im, axis=1
     )

time: 93.6 us -> 83.6 us (0.89)
  other arithmetic: 23.8 us -> 12.8 us
  local copies, waits for them, and re-layouts: 17.1 us -> 8.06 us
  waiting for transfers between devices: 17.8 us -> 24.3 us
  starting transfers between devices: 28.2 us -> 32.3 us
    cos x3 -> x0, other arithmetic: 9.54 us -> none  [the longest x1 4.36 us: segment_tables(): cl, sl = (jnp.cos(low)[:, None, :, :], jnp.sin(low)[:, None, :, :])]
    slice x1 -> x0, local copies, waits for them, and re-layouts: 5.75 us -> none  [shards(): spectra_re, spectra_im = (spectra[:, :, :, 0], spectra[:, :, :, 1])]
    all_to_all x1, waiting for transfers between devices: 8.03 us -> 12.4 us  [shards(): lax.all_to_all(arrival.reshape(pieces, keep, band_rows, seg_len), 'lon',...]
    all_to_all x1, starting transfers between devices: 8.07 us -> 12.2 us  [shards(): lax.all_to_all(arrival.reshape(pieces, keep, band_rows, seg_len), 'lon',...]
    reshape x1 -> x0, local copies, waits for them, and re-layouts: 2.74 us -> none  [shards(): spectra = jnp.einsum('pcrj,rjx->rpcx', gathered, tables, preferred_elemen...]
    ppermute x1, waiting for transfers between devices: 0.01 us -> 2.09 us  [extended(): lax.ppermute(lax.slice_in_dim(block, 0, width, axis=dim), axis, backward)]
  transfers between devices with their start and end apart: 4 -> 4, of which waited for: 2 -> 3; matrix products, arithmetic and copies ran while one was open for 22% -> 11% of each run, Pallas kernels for 0% -> 0%
where the time goes in v4:
time: 83.6 us; the launch traced here: 83.1 us
  starting transfers between devices  32.3 us (39%)
  waiting for transfers between devices  24.3 us (29%)
  other arithmetic  12.8 us (15%)
  local copies, waits for them, and re-layouts  8.06 us (10%)
  matrix products  5.37 us (6%)
    all_to_all x1, starting transfers between devices, shards(): lax.all_to_all(sorted_waves, LAT, split_axis=0, concat_axis=4, tiled=True)  14.9 us
    all_to_all x1, waiting for transfers between devices, shards(): lax.all_to_all(arrival.reshape(pieces, keep, band_rows, seg_len), 'lon',...  12.4 us
    all_to_all x1, starting transfers between devices, shards(): lax.all_to_all(arrival.reshape(pieces, keep, band_rows, seg_len), 'lon',...  12.2 us
    all_to_all x1, waiting for transfers between devices, shards(): lax.all_to_all(sorted_waves, LAT, split_axis=0, concat_axis=4, tiled=True)  9.8 us
    ppermute x1, starting transfers between devices, extended(): lax.ppermute(lax.slice_in_dim(block, block.shape[dim] - width, None, axis...  3.96 us
    convert_element_type x1, other arithmetic, shards(): jnp.where(inside[None], arrival, jnp.float32(0.0)).astype(jnp.bfloat16)  3.64 us
    another operation x1, other arithmetic  2.57 us
    dot_general x1, matrix products, shards(): jnp.einsum('sctl,sln->sctn', sorted_waves, masked_table, preferred_elemen...  2.57 us
  transfers between devices with their start and end apart: 4, of which 3 were waited for; matrix products, arithmetic and copies ran while one was open for 11% of the time, Pallas kernels for 0%

profile of v4, /device:TPU:1, one launch (start us, length us, event | category | flops | bytes accessed | tf_op | source)
XLA Modules:
  0.0 83.1 jit_solution(5726412888808602273)
XLA Ops:
  0.0 0.0 copy-start
  0.0 1.6 %fusion.77 = (bf16[144,3,321]{2,1,0:T(4,128)(2,1)S(1)}, bf16[144,3,321]{2,1,0:T(4,128)(2,1)S(1)}) fusion(bf16[144,4,321]{2,1,0:T(4,128)(2,1)} %param.6), kind=kLoop, calls=%fused_computation.161 | loop fusion | bytes 1109376 | tf_op jit(solution)/shard_map/slice | solution.py:21
  1.6 4.0 %collective-permute-start = (bf16[144,3,321]{2,1,0:T(4,128)(2,1)S(1)}, bf16[144,3,321]{2,1,0:T(4,128)(2,1)S(1)}, u32[]{:S(2)}, u32[]{:S(2)}) collective-permute-start(bf16[144,3,321]{2,1,0:T(4,128)(2,1)S(1)} %get-tuple-element.9), channel_id=1, source_target_pairs={{0,16},{16,32},{32,48},{48,64},{64,80},{80,96},{96,112},{112,128},... | collective-permute-start | bytes 832040 | tf_op jit(solution)/shard_map/ppermute | solution.py:20
  5.6 1.3 %collective-permute-start.1 = (bf16[144,3,321]{2,1,0:T(4,128)(2,1)S(1)}, bf16[144,3,321]{2,1,0:T(4,128)(2,1)S(1)}, u32[]{:S(2)}, u32[]{:S(2)}) collective-permute-start(bf16[144,3,321]{2,1,0:T(4,128)(2,1)S(1)} %get-tuple-element.10), channel_id=1, source_target_pairs={{16,0},{32,16},{48,32},{64,48},{80,64},{96,80},{112,96},{128,112},... | collective-permute-start | bytes 832040 | tf_op jit(solution)/shard_map/ppermute | solution.py:23
  6.9 0.9 %fusion.52 = (f32[4,321]{1,0:T(4,128)S(1)}, f32[4,321]{1,0:T(4,128)S(1)}, f32[4,321]{1,0:T(4,128)S(1)}, f32[4,321]{1,0:T(4,128)S(1)}) fusion(f32[4,4,321]{2,1,0:T(4,128)} %param.7, s32[4,321]{1,0:T(4,128)} %param.8, s32[4]{0:T(128)S(1)} %iota_add_fusion.1), kind=kLoop, calls=%fused_computation.102 | loop fusion | flops 61632 | bytes 46240 | tf_op jit(solution)/shard_map/add | solution.py:79
  7.7 0.8 %fusion.56 = (f32[4,321]{1,0:T(4,128)S(1)}, f32[4,321]{1,0:T(4,128)S(1)}, f32[4,321]{1,0:T(4,128)S(1)}) fusion(f32[4,4,321]{2,1,0:T(4,128)} %param.7, s32[4,321]{1,0:T(4,128)} %param.8, s32[4]{0:T(128)S(1)} %iota_add_fusion.1), kind=kLoop, calls=%fused_computation.106 | loop fusion | flops 47508 | bytes 41104 | tf_op jit(solution)/shard_map/add | solution.py:79
  8.6 0.7 broadcast_divide_fusion
  9.2 0.7 convert_element_type.107
  9.9 0.1 convert_multiply_fusion.1
  10.0 0.1 convert_multiply_fusion.2
  10.1 0.7 broadcast_compare_fusion
  10.8 0.3 negate_select_fusion.4
  11.1 0.7 broadcast_compare_fusion.1
  11.8 0.8 dynamic_slice.3
  12.6 0.3 negate_select_fusion.5
  12.9 0.0 collective-permute-done
  12.9 2.1 %collective-permute-done.1 = bf16[144,3,321]{2,1,0:T(4,128)(2,1)S(1)} collective-permute-done((bf16[144,3,321]{2,1,0:T(4,128)(2,1)S(1)}, bf16[144,3,321]{2,1,0:T(4,128)(2,1)S(1)}, u32[]{:S(2)}, u32[]{:S(2)}) %collective-permute-start.1) | collective-permute-done | bytes 277376 | tf_op jit(solution)/shard_map/ppermute | solution.py:23
  15.0 0.0 copy-done
  15.0 3.6 %select_convert_fusion = bf16[144,4,321]{2,1,0:T(4,128)(2,1)} fusion(bf16[144,4,321]{2,1,0:T(4,128)(2,1)S(1)} %copy-done, bf16[144,3,321]{2,1,0:T(4,128)(2,1)S(1)} %collective-permute-done.1, bf16[144,3,321]{2,1,0:T(4,128)(2,1)S(1)} %collective-permute-done, f32[4,321]{1,0:T(4,128)S(1)} %get-tuple-element.23, f32[4,321]{1,0:T(4,128)S(1)} %get-tuple-element.22, ...), kind=kLoop, calls=%fused_computation.27 | loop fusion | flops 7395840 | bytes 1331508 | tf_op jit(solution)/shard_map/convert_element_type | solution.py:86
  18.6 12.2 %all-to-all-start = ((bf16[16,9,4,321]{3,2,1,0:T(4,128)(2,1)}), bf16[16,9,4,321]{3,2,1,0:T(4,128)(2,1)S(1)}, u32[]{:S(2)}, u32[]{:S(2)}) async-start(bf16[16,9,4,321]{3,2,1,0:T(4,128)(2,1)} %bitcast.6), calls=%async_computation | async-start | bytes 884736 | tf_op jit(solution)/shard_map/all_to_all | solution.py:87
  30.8 0.5 negate_select_fusion.1
  31.3 2.6 %subtract_convert_fusion = (bf16[4,11,32,640]{3,2,1,0:T(8,128)(2,1)S(1)}, bf16[4,11,32,640]{3,2,1,0:T(8,128)(2,1)}) fusion(f32[4,32,640]{2,1,0:T(8,128)S(1)} %get-tuple-element.12, f32[4,11,640]{2,1,0:T(8,128)S(1)} %get-tuple-element.16, f32[4,32,640]{2,1,0:T(8,128)S(1)} %get-tuple-element.11, f32[4,11,640]{2,1,0:T(8,128)S(1)} %get-tuple-element.15), kind=kLoop, calls=%fused_computation.1 | loop fusion | flops 8110080 | bytes 4485120 | tf_op jit(solution)/shard_map/convert.3
  33.9 12.4 %all-to-all-done = bf16[16,9,4,321]{3,2,1,0:T(4,128)(2,1)S(1)} async-done(((bf16[16,9,4,321]{3,2,1,0:T(4,128)(2,1)}), bf16[16,9,4,321]{3,2,1,0:T(4,128)(2,1)S(1)}, u32[]{:S(2)}, u32[]{:S(2)}) %all-to-all-start) | async-done | bytes 369824 | tf_op jit(solution)/shard_map/all_to_all | solution.py:87
  46.3 2.4 %fusion.1 = f32[4,16,9,1280]{3,1,2,0:T(8,128)S(1)} fusion(bf16[4,352,640]{2,1,0:T(8,128)(2,1)} %bitcast.158, bf16[4,352,640]{2,1,0:T(8,128)(2,1)S(1)} %bitcast.157, bf16[16,9,4,321]{3,2,1,0:T(4,128)(2,1)S(1)} %all-to-all-done), kind=kOutput, calls=%fused_computation.4 | convolution fusion | flops 479907840 | bytes 6923392 | tf_op jit(solution)/shard_map/pcrj,rjx->rpcx/dot_general | solution.py:93
  48.7 0.0 copy-start.1
  48.7 0.8 subtract_reduce_fusion
  49.5 0.0 copy-done.1
  49.5 0.4 fusion.18
  49.9 1.4 %reshape.330 = bf16[32,20,9,2,4]{1,0,2,3,4:T(8,128)(2,1)S(1)} reshape(bf16[640,9,2,4]{0,1,2,3:T(8,128)(2,1)S(1)} %fusion.18) | data formatting | bytes 184320 | tf_op jit(solution)/shard_map/reshape | solution.py:116
  51.4 0.5 copy.35
  51.9 1.4 %reshape.331 = bf16[32,2,720]{2,1,0:T(2,128)(2,1)} reshape(bf16[32,9,2,4,20]{4,3,2,1,0:T(4,128)(2,1)S(1)} %bitcast.159) | data formatting | bytes 184320
  53.2 14.9 %all-to-all-start.1 = ((bf16[32,2,720]{2,1,0:T(2,128)(2,1)}), bf16[32,2,720]{2,1,0:T(2,128)(2,1)S(1)}, u32[]{:S(2)}, u32[]{:S(2)}) async-start(bf16[32,2,720]{2,1,0:T(2,128)(2,1)} %reshape.331), calls=%async_computation.1 | async-start | bytes 196608 | tf_op jit(solution)/shard_map/all_to_all | solution.py:117
  68.1 0.1 iota_compare_fusion.1
  68.2 9.8 %all-to-all-done.1 = bf16[32,2,720]{2,1,0:T(2,128)(2,1)S(1)} async-done(((bf16[32,2,720]{2,1,0:T(2,128)(2,1)}), bf16[32,2,720]{2,1,0:T(2,128)(2,1)S(1)}, u32[]{:S(2)}, u32[]{:S(2)}) %all-to-all-start.1) | async-done | bytes 92192 | tf_op jit(solution)/shard_map/all_to_all | solution.py:117
  78.0 0.4 reshape.332
  78.4 0.2 bitcast_bitcast_fusion
  78.6 0.3 copy.24
  78.9 0.5 copy.25
  79.3 2.6 %fusion.12 = bf16[20,9,2,640]{3,1,2,0:T(8,128)(2,1)S(1)} fusion(bf16[20,9,2,128]{3,1,2,0:T(8,128)(2,1)S(1)} %copy.25, bf16[20,128,640]{2,1,0:T(8,128)(2,1)} %param.11, pred[20,640]{1,0:T(8,128)(4,1)S(1)} %iota_compare_fusion.1), kind=kOutput, calls=%fused_computation.16 | convolution fusion | flops 60851200 | bytes 3842560 | tf_op jit(solution)/shard_map/sctl,sln->sctn/dot_general | solution.py:123
  81.9 1.1 %copy.26 = bf16[20,9,2,640]{3,2,1,0:T(2,128)(2,1)} copy(bf16[20,9,2,640]{3,1,2,0:T(8,128)(2,1)S(1)} %fusion.12) | data formatting | bytes 921600 | tf_op jit(solution)/shard_map/convert_element_type | solution.py:126
  (6 shorter events, 0.0 us)
Async XLA Ops:
  0.0 15.0 %copy-start = (bf16[144,4,321]{2,1,0:T(4,128)(2,1)S(1)}, bf16[144,4,321]{2,1,0:T(4,128)(2,1)}, u32[]{:S(2)}) copy-start(bf16[144,4,321]{2,1,0:T(4,128)(2,1)} %param.6) | copy-start | bytes 1109380
  1.6 11.3 %collective-permute-start = (bf16[144,3,321]{2,1,0:T(4,128)(2,1)S(1)}, bf16[144,3,321]{2,1,0:T(4,128)(2,1)S(1)}, u32[]{:S(2)}, u32[]{:S(2)}) collective-permute-start(bf16[144,3,321]{2,1,0:T(4,128)(2,1)S(1)} %get-tuple-element.9), channel_id=1, source_target_pairs={{0,16},{16,32},{32,48},{48,64},{64,80},{80,96},{96,112},{112,128},... | collective-permute-start | bytes 832040 | tf_op jit(solution)/shard_map/ppermute | solution.py:20
  5.6 9.4 %collective-permute-start.1 = (bf16[144,3,321]{2,1,0:T(4,128)(2,1)S(1)}, bf16[144,3,321]{2,1,0:T(4,128)(2,1)S(1)}, u32[]{:S(2)}, u32[]{:S(2)}) collective-permute-start(bf16[144,3,321]{2,1,0:T(4,128)(2,1)S(1)} %get-tuple-element.10), channel_id=1, source_target_pairs={{16,0},{32,16},{48,32},{64,48},{80,64},{96,80},{112,96},{128,112},... | collective-permute-start | bytes 832040 | tf_op jit(solution)/shard_map/ppermute | solution.py:23
  18.6 27.7 %all-to-all-start = ((bf16[16,9,4,321]{3,2,1,0:T(4,128)(2,1)}), bf16[16,9,4,321]{3,2,1,0:T(4,128)(2,1)S(1)}, u32[]{:S(2)}, u32[]{:S(2)}) async-start(bf16[16,9,4,321]{3,2,1,0:T(4,128)(2,1)} %bitcast.6), calls=%async_computation | async-start | bytes 884736 | tf_op jit(solution)/shard_map/all_to_all | solution.py:87
  48.7 0.8 copy-start.1
  53.2 24.8 %all-to-all-start.1 = ((bf16[32,2,720]{2,1,0:T(2,128)(2,1)}), bf16[32,2,720]{2,1,0:T(2,128)(2,1)S(1)}, u32[]{:S(2)}, u32[]{:S(2)}) async-start(bf16[32,2,720]{2,1,0:T(2,128)(2,1)} %reshape.331), calls=%async_computation.1 | async-start | bytes 196608 | tf_op jit(solution)/shard_map/all_to_all | solution.py:117

commit v5 on v4

--- a/solution.py
+++ b/solution.py
@@ -108,12 +108,11 @@
         resolved[:, None, None, :], fourier * inverse[:, None, None, None], jnp.float32(0.0)
     )
     fourier = fourier.astype(jnp.bfloat16)
-    pick = (wave_order[None, :] == wavenumber[:, None]).astype(jnp.bfloat16)
+    count = lax.axis_size(LAT)
+    pick = (wave_order[None, :] == wavenumber[:, None]).astype(jnp.bfloat16).reshape(M, count, slots)
     sorted_waves = jnp.einsum(
-        "rctm,ms->sctr", fourier, pick, preferred_element_type=jnp.float32
+        "rctm,mqs->qsctr", fourier, pick, preferred_element_type=jnp.float32
     ).astype(jnp.bfloat16)
-    count = lax.axis_size(LAT)
-    sorted_waves = sorted_waves.reshape((count, slots) + sorted_waves.shape[1:])
     sorted_waves = lax.all_to_all(sorted_waves, LAT, split_axis=0, concat_axis=4, tiled=True)[0]
     my_slots = lax.dynamic_slice_in_dim(wave_order, lax.axis_index(LAT) * slots, slots)
     degree = jnp.arange(NDEG, dtype=jnp.int32)

time: 83.6 us -> 83.1 us (level)
    reshape x2 -> x0, local copies, waits for them, and re-layouts: 1.9 us -> none  [shards(): sorted_waves = sorted_waves.reshape((count, slots) + sorted_waves.shape[1:])]
    convert_element_type x0 -> x1, local copies, waits for them, and re-layouts: none -> 0.94 us  [shards(): sorted_waves = jnp.einsum('rctm,mqs->qsctr', fourier, pick, preferred_ele...]
    ppermute x1, waiting for transfers between devices: 2.09 us -> 1.21 us  [extended(): lax.ppermute(lax.slice_in_dim(block, 0, width, axis=dim), axis, backward)]
    eq x0 -> x2, local copies, waits for them, and re-layouts: none -> 0.86 us  [shards(): wave_order[None, :] == wavenumber[:, None]]
    unnamed x6 -> x4, local copies, waits for them, and re-layouts: 1.74 us -> 1.74 us
  transfers between devices with their start and end apart: 4 -> 4, of which waited for: 3 -> 3; matrix products, arithmetic and copies ran while one was open for 11% -> 12% of each run, Pallas kernels for 0% -> 0%
where the time goes in v5:
time: 83.1 us; the launch traced here: 82.6 us
  starting transfers between devices  32.3 us (39%)
  waiting for transfers between devices  23.5 us (28%)
  other arithmetic  12.8 us (15%)
  local copies, waits for them, and re-layouts  7.96 us (10%)
  matrix products  5.9 us (7%)
    all_to_all x1, starting transfers between devices, shards(): lax.all_to_all(sorted_waves, LAT, split_axis=0, concat_axis=4, tiled=True)  14.9 us
    all_to_all x1, waiting for transfers between devices, shards(): lax.all_to_all(arrival.reshape(pieces, keep, band_rows, seg_len), 'lon',...  12.4 us
    all_to_all x1, starting transfers between devices, shards(): lax.all_to_all(arrival.reshape(pieces, keep, band_rows, seg_len), 'lon',...  12.2 us
    all_to_all x1, waiting for transfers between devices, shards(): lax.all_to_all(sorted_waves, LAT, split_axis=0, concat_axis=4, tiled=True)  9.8 us
    ppermute x1, starting transfers between devices, extended(): lax.ppermute(lax.slice_in_dim(block, block.shape[dim] - width, None, axis...  3.96 us
    convert_element_type x1, other arithmetic, shards(): jnp.where(inside[None], arrival, jnp.float32(0.0)).astype(jnp.bfloat16)  3.64 us
    dot_general x1, matrix products, shards(): jnp.einsum('sctl,sln->sctn', sorted_waves, masked_table, preferred_elemen...  2.57 us
    another operation x1, other arithmetic  2.56 us
  transfers between devices with their start and end apart: 4, of which 3 were waited for; matrix products, arithmetic and copies ran while one was open for 12% of the time, Pallas kernels for 0%

profile of v5, /device:TPU:1, one launch (start us, length us, event | category | flops | bytes accessed | tf_op | source)
XLA Modules:
  0.0 82.6 jit_solution(13036687852906643935)
XLA Ops:
  0.0 0.0 copy-start
  0.0 1.6 %fusion.78 = (bf16[144,3,321]{2,1,0:T(4,128)(2,1)S(1)}, bf16[144,3,321]{2,1,0:T(4,128)(2,1)S(1)}) fusion(bf16[144,4,321]{2,1,0:T(4,128)(2,1)} %param.6), kind=kLoop, calls=%fused_computation.162 | loop fusion | bytes 1109376 | tf_op jit(solution)/shard_map/slice | solution.py:21
  1.6 4.0 %collective-permute-start = (bf16[144,3,321]{2,1,0:T(4,128)(2,1)S(1)}, bf16[144,3,321]{2,1,0:T(4,128)(2,1)S(1)}, u32[]{:S(2)}, u32[]{:S(2)}) collective-permute-start(bf16[144,3,321]{2,1,0:T(4,128)(2,1)S(1)} %get-tuple-element.9), channel_id=1, source_target_pairs={{0,16},{16,32},{32,48},{48,64},{64,80},{80,96},{96,112},{112,128},... | collective-permute-start | bytes 832040 | tf_op jit(solution)/shard_map/ppermute | solution.py:20
  5.6 1.3 %collective-permute-start.1 = (bf16[144,3,321]{2,1,0:T(4,128)(2,1)S(1)}, bf16[144,3,321]{2,1,0:T(4,128)(2,1)S(1)}, u32[]{:S(2)}, u32[]{:S(2)}) collective-permute-start(bf16[144,3,321]{2,1,0:T(4,128)(2,1)S(1)} %get-tuple-element.10), channel_id=1, source_target_pairs={{16,0},{32,16},{48,32},{64,48},{80,64},{96,80},{112,96},{128,112},... | collective-permute-start | bytes 832040 | tf_op jit(solution)/shard_map/ppermute | solution.py:23
  6.9 0.9 %fusion.53 = (f32[4,321]{1,0:T(4,128)S(1)}, f32[4,321]{1,0:T(4,128)S(1)}, f32[4,321]{1,0:T(4,128)S(1)}, f32[4,321]{1,0:T(4,128)S(1)}) fusion(f32[4,4,321]{2,1,0:T(4,128)} %param.7, s32[4,321]{1,0:T(4,128)} %param.8, s32[4]{0:T(128)S(1)} %iota_add_fusion.1), kind=kLoop, calls=%fused_computation.103 | loop fusion | flops 61632 | bytes 46240 | tf_op jit(solution)/shard_map/add | solution.py:79
  7.7 0.8 %fusion.57 = (f32[4,321]{1,0:T(4,128)S(1)}, f32[4,321]{1,0:T(4,128)S(1)}, f32[4,321]{1,0:T(4,128)S(1)}) fusion(f32[4,4,321]{2,1,0:T(4,128)} %param.7, s32[4,321]{1,0:T(4,128)} %param.8, s32[4]{0:T(128)S(1)} %iota_add_fusion.1), kind=kLoop, calls=%fused_computation.107 | loop fusion | flops 47508 | bytes 41104 | tf_op jit(solution)/shard_map/add | solution.py:79
  8.6 0.7 broadcast_divide_fusion
  9.2 0.7 convert_element_type.107
  9.9 0.1 convert_multiply_fusion.1
  10.0 0.1 convert_multiply_fusion.2
  10.1 0.7 broadcast_compare_fusion
  10.8 0.3 negate_select_fusion.4
  11.1 0.7 broadcast_compare_fusion.1
  11.8 0.8 eq.172
  12.6 0.1 copy.20
  12.7 0.8 dynamic_slice.3
  13.5 0.3 negate_select_fusion.5
  13.8 0.0 collective-permute-done
  13.8 1.2 %collective-permute-done.1 = bf16[144,3,321]{2,1,0:T(4,128)(2,1)S(1)} collective-permute-done((bf16[144,3,321]{2,1,0:T(4,128)(2,1)S(1)}, bf16[144,3,321]{2,1,0:T(4,128)(2,1)S(1)}, u32[]{:S(2)}, u32[]{:S(2)}) %collective-permute-start.1) | collective-permute-done | bytes 277376 | tf_op jit(solution)/shard_map/ppermute | solution.py:23
  15.0 0.0 copy-done
  15.0 3.6 %select_convert_fusion = bf16[144,4,321]{2,1,0:T(4,128)(2,1)} fusion(bf16[144,4,321]{2,1,0:T(4,128)(2,1)S(1)} %copy-done, bf16[144,3,321]{2,1,0:T(4,128)(2,1)S(1)} %collective-permute-done.1, bf16[144,3,321]{2,1,0:T(4,128)(2,1)S(1)} %collective-permute-done, f32[4,321]{1,0:T(4,128)S(1)} %get-tuple-element.23, f32[4,321]{1,0:T(4,128)S(1)} %get-tuple-element.22, ...), kind=kLoop, calls=%fused_computation.27 | loop fusion | flops 7395840 | bytes 1331508 | tf_op jit(solution)/shard_map/convert_element_type | solution.py:86
  18.6 12.2 %all-to-all-start = ((bf16[16,9,4,321]{3,2,1,0:T(4,128)(2,1)}), bf16[16,9,4,321]{3,2,1,0:T(4,128)(2,1)S(1)}, u32[]{:S(2)}, u32[]{:S(2)}) async-start(bf16[16,9,4,321]{3,2,1,0:T(4,128)(2,1)} %bitcast.6), calls=%async_computation | async-start | bytes 884736 | tf_op jit(solution)/shard_map/all_to_all | solution.py:87
  30.8 0.5 negate_select_fusion.1
  31.3 2.6 %subtract_convert_fusion = (bf16[4,11,32,640]{3,2,1,0:T(8,128)(2,1)S(1)}, bf16[4,11,32,640]{3,2,1,0:T(8,128)(2,1)}) fusion(f32[4,32,640]{2,1,0:T(8,128)S(1)} %get-tuple-element.12, f32[4,11,640]{2,1,0:T(8,128)S(1)} %get-tuple-element.16, f32[4,32,640]{2,1,0:T(8,128)S(1)} %get-tuple-element.11, f32[4,11,640]{2,1,0:T(8,128)S(1)} %get-tuple-element.15), kind=kLoop, calls=%fused_computation.1 | loop fusion | flops 8110080 | bytes 4485120 | tf_op jit(solution)/shard_map/convert.3
  33.9 12.4 %all-to-all-done = bf16[16,9,4,321]{3,2,1,0:T(4,128)(2,1)S(1)} async-done(((bf16[16,9,4,321]{3,2,1,0:T(4,128)(2,1)}), bf16[16,9,4,321]{3,2,1,0:T(4,128)(2,1)S(1)}, u32[]{:S(2)}, u32[]{:S(2)}) %all-to-all-start) | async-done | bytes 369824 | tf_op jit(solution)/shard_map/all_to_all | solution.py:87
  46.3 2.4 %fusion.1 = f32[4,16,9,1280]{3,1,2,0:T(8,128)S(1)} fusion(bf16[4,352,640]{2,1,0:T(8,128)(2,1)} %bitcast.157, bf16[4,352,640]{2,1,0:T(8,128)(2,1)S(1)} %bitcast.156, bf16[16,9,4,321]{3,2,1,0:T(4,128)(2,1)S(1)} %all-to-all-done), kind=kOutput, calls=%fused_computation.4 | convolution fusion | flops 479907840 | bytes 6923392 | tf_op jit(solution)/shard_map/pcrj,rjx->rpcx/dot_general | solution.py:93
  48.7 0.8 subtract_reduce_fusion
  49.5 1.0 %fusion.18 = bf16[32,20,9,2,4]{0,2,3,4,1:T(8,128)(2,1)S(1)} fusion(s32[32,20]{0,1:T(8,128)S(1)} %copy.20, f32[4,9,1,640]{3,1,2,0:T(8,128)S(1)} %bitcast.161, f32[4,9,1,640]{3,1,2,0:T(8,128)S(1)} %bitcast.160, f32[4]{0:T(128)S(1)} %get-tuple-element.25, pred[4,640]{1,0:T(4,128)(4,1)S(1)} %broadcast_compare_fusion), kind=kOutput, calls=%fused_computation.18 | convolution fusion | flops 59622400 | bytes 281616 | tf_op jit(solution)/shard_map/rctm,mqs->qsctr/dot_general | solution.py:113
  50.4 0.9 %copy.22 = bf16[32,20,9,2,4]{1,4,3,2,0:T(4,128)(2,1)S(1)} copy(bf16[32,20,9,2,4]{0,2,3,4,1:T(8,128)(2,1)S(1)} %fusion.18) | data formatting | bytes 184320 | tf_op jit(solution)/shard_map/convert_element_type | solution.py:115
  51.4 1.4 %reshape.336 = bf16[32,2,720]{2,1,0:T(2,128)(2,1)} reshape(bf16[32,9,2,4,20]{4,3,2,1,0:T(4,128)(2,1)S(1)} %bitcast.158) | data formatting | bytes 184320
  52.7 14.9 %all-to-all-start.1 = ((bf16[32,2,720]{2,1,0:T(2,128)(2,1)}), bf16[32,2,720]{2,1,0:T(2,128)(2,1)S(1)}, u32[]{:S(2)}, u32[]{:S(2)}) async-start(bf16[32,2,720]{2,1,0:T(2,128)(2,1)} %reshape.336), calls=%async_computation.1 | async-start | bytes 196608 | tf_op jit(solution)/shard_map/all_to_all | solution.py:116
  67.6 0.1 iota_compare_fusion.1
  67.7 9.8 %all-to-all-done.1 = bf16[32,2,720]{2,1,0:T(2,128)(2,1)S(1)} async-done(((bf16[32,2,720]{2,1,0:T(2,128)(2,1)}), bf16[32,2,720]{2,1,0:T(2,128)(2,1)S(1)}, u32[]{:S(2)}, u32[]{:S(2)}) %all-to-all-start.1) | async-done | bytes 92192 | tf_op jit(solution)/shard_map/all_to_all | solution.py:116
  77.5 0.4 reshape.337
  77.9 0.2 bitcast_bitcast_fusion
  78.1 0.3 copy.23
  78.4 0.5 copy.24
  78.9 2.6 %fusion.12 = bf16[20,9,2,640]{3,1,2,0:T(8,128)(2,1)S(1)} fusion(bf16[20,9,2,128]{3,1,2,0:T(8,128)(2,1)S(1)} %copy.24, bf16[20,128,640]{2,1,0:T(8,128)(2,1)} %param.11, pred[20,640]{1,0:T(8,128)(4,1)S(1)} %iota_compare_fusion.1), kind=kOutput, calls=%fused_computation.16 | convolution fusion | flops 60851200 | bytes 3842560 | tf_op jit(solution)/shard_map/sctl,sln->sctn/dot_general | solution.py:122
  81.4 1.1 %copy.25 = bf16[20,9,2,640]{3,2,1,0:T(2,128)(2,1)} copy(bf16[20,9,2,640]{3,1,2,0:T(8,128)(2,1)S(1)} %fusion.12) | data formatting | bytes 921600 | tf_op jit(solution)/shard_map/convert_element_type | solution.py:125
  (6 shorter events, 0.0 us)
Async XLA Ops:
  0.0 15.0 %copy-start = (bf16[144,4,321]{2,1,0:T(4,128)(2,1)S(1)}, bf16[144,4,321]{2,1,0:T(4,128)(2,1)}, u32[]{:S(2)}) copy-start(bf16[144,4,321]{2,1,0:T(4,128)(2,1)} %param.6) | copy-start | bytes 1109380
  1.6 12.2 %collective-permute-start = (bf16[144,3,321]{2,1,0:T(4,128)(2,1)S(1)}, bf16[144,3,321]{2,1,0:T(4,128)(2,1)S(1)}, u32[]{:S(2)}, u32[]{:S(2)}) collective-permute-start(bf16[144,3,321]{2,1,0:T(4,128)(2,1)S(1)} %get-tuple-element.9), channel_id=1, source_target_pairs={{0,16},{16,32},{32,48},{48,64},{64,80},{80,96},{96,112},{112,128},... | collective-permute-start | bytes 832040 | tf_op jit(solution)/shard_map/ppermute | solution.py:20
  5.6 9.4 %collective-permute-start.1 = (bf16[144,3,321]{2,1,0:T(4,128)(2,1)S(1)}, bf16[144,3,321]{2,1,0:T(4,128)(2,1)S(1)}, u32[]{:S(2)}, u32[]{:S(2)}) collective-permute-start(bf16[144,3,321]{2,1,0:T(4,128)(2,1)S(1)} %get-tuple-element.10), channel_id=1, source_target_pairs={{16,0},{32,16},{48,32},{64,48},{80,64},{96,80},{112,96},{128,112},... | collective-permute-start | bytes 832040 | tf_op jit(solution)/shard_map/ppermute | solution.py:23
  18.6 27.7 %all-to-all-start = ((bf16[16,9,4,321]{3,2,1,0:T(4,128)(2,1)}), bf16[16,9,4,321]{3,2,1,0:T(4,128)(2,1)S(1)}, u32[]{:S(2)}, u32[]{:S(2)}) async-start(bf16[16,9,4,321]{3,2,1,0:T(4,128)(2,1)} %bitcast.6), calls=%async_computation | async-start | bytes 884736 | tf_op jit(solution)/shard_map/all_to_all | solution.py:87
  52.7 24.8 %all-to-all-start.1 = ((bf16[32,2,720]{2,1,0:T(2,128)(2,1)}), bf16[32,2,720]{2,1,0:T(2,128)(2,1)S(1)}, u32[]{:S(2)}, u32[]{:S(2)}) async-start(bf16[32,2,720]{2,1,0:T(2,128)(2,1)} %reshape.336), calls=%async_computation.1 | async-start | bytes 196608 | tf_op jit(solution)/shard_map/all_to_all | solution.py:116

commit v6 on v5

--- a/solution.py
+++ b/solution.py
@@ -17,11 +17,13 @@
         count = lax.axis_size(axis)
         forward = [(i, i + 1) for i in range(count - 1)]
         backward = [(target, source) for source, target in forward]
-        low = lax.ppermute(
-            lax.slice_in_dim(block, block.shape[dim] - width, None, axis=dim), axis, forward
+        low = lax.ppermute(block, axis, forward)
+        high = lax.ppermute(block, axis, backward)
+        size = block.shape[dim]
+        block = jnp.concatenate(
+            [lax.slice_in_dim(low, size - width, None, axis=dim), block, lax.slice_in_dim(high, 0, width, axis=dim)],
+            axis=dim,
         )
-        high = lax.ppermute(lax.slice_in_dim(block, 0, width, axis=dim), axis, backward)
-        block = jnp.concatenate([low, block, high], axis=dim)
     return block
 
 

time: 83.1 us -> 84.7 us (1.019)
  other arithmetic: 12.8 us -> 15.7 us
  local copies, waits for them, and re-layouts: 7.96 us -> 6.61 us
    convert_element_type x1, other arithmetic: 3.64 us -> 6.46 us  [shards(): jnp.where(inside[None], arrival, jnp.float32(0.0)).astype(jnp.bfloat16)]
    slice x1, local copies, waits for them, and re-layouts: 1.58 us -> 0.24 us  [extended(): lax.slice_in_dim(low, size - width, None, axis=dim)]
    unnamed x4 -> x2, local copies, waits for them, and re-layouts: 1.74 us -> 1.73 us
where the time goes in v6:
time: 84.7 us; the launch traced here: 84.1 us
  starting transfers between devices  32.2 us (38%)
  waiting for transfers between devices  23.4 us (28%)
  other arithmetic  15.7 us (19%)
  local copies, waits for them, and re-layouts  6.61 us (8%)
  matrix products  5.99 us (7%)
    all_to_all x1, starting transfers between devices, shards(): lax.all_to_all(sorted_waves, LAT, split_axis=0, concat_axis=4, tiled=True)  14.8 us
    all_to_all x1, waiting for transfers between devices, shards(): lax.all_to_all(arrival.reshape(pieces, keep, band_rows, seg_len), 'lon',...  12.4 us
    all_to_all x1, starting transfers between devices, shards(): lax.all_to_all(arrival.reshape(pieces, keep, band_rows, seg_len), 'lon',...  12.2 us
    all_to_all x1, waiting for transfers between devices, shards(): lax.all_to_all(sorted_waves, LAT, split_axis=0, concat_axis=4, tiled=True)  9.82 us
    convert_element_type x1, other arithmetic, shards(): jnp.where(inside[None], arrival, jnp.float32(0.0)).astype(jnp.bfloat16)  6.46 us
    ppermute x1, starting transfers between devices, extended(): low = lax.ppermute(block, axis, forward)  3.95 us
    another operation x1, other arithmetic  2.61 us
    dot_general x1, matrix products, shards(): jnp.einsum('sctl,sln->sctn', sorted_waves, masked_table, preferred_elemen...  2.58 us
  transfers between devices with their start and end apart: 4, of which 3 were waited for; matrix products, arithmetic and copies ran while one was open for 12% of the time, Pallas kernels for 0%

profile of v6, /device:TPU:1, one launch (start us, length us, event | category | flops | bytes accessed | tf_op | source)
XLA Modules:
  0.0 84.1 jit_solution(7131223151160695008)
XLA Ops:
  0.0 4.0 %collective-permute-start = (bf16[144,4,321]{2,1,0:T(4,128)(2,1)}, bf16[144,4,321]{2,1,0:T(4,128)(2,1)S(1)}, u32[]{:S(2)}, u32[]{:S(2)}) collective-permute-start(bf16[144,4,321]{2,1,0:T(4,128)(2,1)} %param.6), channel_id=1, source_target_pairs={{0,16},{16,32},{32,48},{48,64},{64,80},{80,96},{96,112},{112,128},... | collective-permute-start | bytes 1109384 | tf_op jit(solution)/shard_map/ppermute | solution.py:20
  4.0 1.3 %collective-permute-start.1 = (bf16[144,4,321]{2,1,0:T(4,128)(2,1)}, bf16[144,4,321]{2,1,0:T(4,128)(2,1)S(1)}, u32[]{:S(2)}, u32[]{:S(2)}) collective-permute-start(bf16[144,4,321]{2,1,0:T(4,128)(2,1)} %param.6), channel_id=1, source_target_pairs={{16,0},{32,16},{48,32},{64,48},{80,64},{96,80},{112,96},{128,112},... | collective-permute-start | bytes 1109384 | tf_op jit(solution)/shard_map/ppermute | solution.py:21
  5.3 0.9 %fusion.53 = (f32[4,321]{1,0:T(4,128)S(1)}, f32[4,321]{1,0:T(4,128)S(1)}, f32[4,321]{1,0:T(4,128)S(1)}, f32[4,321]{1,0:T(4,128)S(1)}) fusion(f32[4,4,321]{2,1,0:T(4,128)} %param.7, s32[4,321]{1,0:T(4,128)} %param.8, s32[4]{0:T(128)S(1)} %iota_add_fusion.1), kind=kLoop, calls=%fused_computation.103 | loop fusion | flops 61632 | bytes 46240 | tf_op jit(solution)/shard_map/add | solution.py:81
  6.1 0.8 %fusion.57 = (f32[4,321]{1,0:T(4,128)S(1)}, f32[4,321]{1,0:T(4,128)S(1)}, f32[4,321]{1,0:T(4,128)S(1)}) fusion(f32[4,4,321]{2,1,0:T(4,128)} %param.7, s32[4,321]{1,0:T(4,128)} %param.8, s32[4]{0:T(128)S(1)} %iota_add_fusion.1), kind=kLoop, calls=%fused_computation.107 | loop fusion | flops 47508 | bytes 41104 | tf_op jit(solution)/shard_map/add | solution.py:81
  7.0 0.7 broadcast_divide_fusion
  7.6 0.7 convert_element_type.107
  8.3 0.1 convert_multiply_fusion.1
  8.4 0.1 convert_multiply_fusion.2
  8.5 0.8 eq.172
  9.3 0.1 copy.20
  9.4 0.7 broadcast_compare_fusion
  10.1 0.8 dynamic_slice.3
  10.9 0.3 negate_select_fusion.4
  11.1 0.7 broadcast_compare_fusion.1
  11.9 0.3 negate_select_fusion.5
  12.2 0.0 collective-permute-done
  12.2 0.2 slice.90
  12.4 1.2 %collective-permute-done.1 = bf16[144,4,321]{2,1,0:T(4,128)(2,1)S(1)} collective-permute-done((bf16[144,4,321]{2,1,0:T(4,128)(2,1)}, bf16[144,4,321]{2,1,0:T(4,128)(2,1)S(1)}, u32[]{:S(2)}, u32[]{:S(2)}) %collective-permute-start.1) | collective-permute-done | bytes 369824 | tf_op jit(solution)/shard_map/ppermute | solution.py:21
  13.6 6.5 %select_convert_fusion = bf16[144,4,321]{2,1,0:T(4,128)(2,1)} fusion(bf16[144,4,321]{2,1,0:T(4,128)(2,1)} %param.6, bf16[144,3,321]{2,1,0:T(4,128)(2,1)S(1)} %bitcast.161, bf16[144,3,321]{2,1,0:T(4,128)(2,1)S(1)} %slice.90, f32[4,321]{1,0:T(4,128)S(1)} %get-tuple-element.21, f32[4,321]{1,0:T(4,128)S(1)} %get-tuple-element.20, ...), kind=kLoop, calls=%fused_computation.27 | loop fusion | flops 7395840 | bytes 1331508 | tf_op jit(solution)/shard_map/convert_element_type | solution.py:88
  20.1 12.2 %all-to-all-start = ((bf16[16,9,4,321]{3,2,1,0:T(4,128)(2,1)}), bf16[16,9,4,321]{3,2,1,0:T(4,128)(2,1)S(1)}, u32[]{:S(2)}, u32[]{:S(2)}) async-start(bf16[16,9,4,321]{3,2,1,0:T(4,128)(2,1)} %bitcast.6), calls=%async_computation | async-start | bytes 884736 | tf_op jit(solution)/shard_map/all_to_all | solution.py:89
  32.2 0.5 negate_select_fusion.1
  32.7 2.6 %subtract_convert_fusion = (bf16[4,11,32,640]{3,2,1,0:T(8,128)(2,1)S(1)}, bf16[4,11,32,640]{3,2,1,0:T(8,128)(2,1)}) fusion(f32[4,32,640]{2,1,0:T(8,128)S(1)} %get-tuple-element.10, f32[4,11,640]{2,1,0:T(8,128)S(1)} %get-tuple-element.14, f32[4,32,640]{2,1,0:T(8,128)S(1)} %get-tuple-element.9, f32[4,11,640]{2,1,0:T(8,128)S(1)} %get-tuple-element.13), kind=kLoop, calls=%fused_computation.1 | loop fusion | flops 8110080 | bytes 4485120 | tf_op jit(solution)/shard_map/convert.3
  35.3 12.4 %all-to-all-done = bf16[16,9,4,321]{3,2,1,0:T(4,128)(2,1)S(1)} async-done(((bf16[16,9,4,321]{3,2,1,0:T(4,128)(2,1)}), bf16[16,9,4,321]{3,2,1,0:T(4,128)(2,1)S(1)}, u32[]{:S(2)}, u32[]{:S(2)}) %all-to-all-start) | async-done | bytes 369824 | tf_op jit(solution)/shard_map/all_to_all | solution.py:89
  47.7 2.4 %fusion.1 = f32[4,16,9,1280]{3,1,2,0:T(8,128)S(1)} fusion(bf16[4,352,640]{2,1,0:T(8,128)(2,1)} %bitcast.158, bf16[4,352,640]{2,1,0:T(8,128)(2,1)S(1)} %bitcast.157, bf16[16,9,4,321]{3,2,1,0:T(4,128)(2,1)S(1)} %all-to-all-done), kind=kOutput, calls=%fused_computation.4 | convolution fusion | flops 479907840 | bytes 6923392 | tf_op jit(solution)/shard_map/pcrj,rjx->rpcx/dot_general | solution.py:95
  50.2 0.8 subtract_reduce_fusion
  51.0 1.0 %fusion.18 = bf16[32,20,9,2,4]{0,2,3,4,1:T(8,128)(2,1)S(1)} fusion(s32[32,20]{0,1:T(8,128)S(1)} %copy.20, f32[4,9,1,640]{3,1,2,0:T(8,128)S(1)} %bitcast.163, f32[4,9,1,640]{3,1,2,0:T(8,128)S(1)} %bitcast.162, f32[4]{0:T(128)S(1)} %get-tuple-element.23, pred[4,640]{1,0:T(4,128)(4,1)S(1)} %broadcast_compare_fusion), kind=kOutput, calls=%fused_computation.18 | convolution fusion | flops 59622400 | bytes 281616 | tf_op jit(solution)/shard_map/rctm,mqs->qsctr/dot_general | solution.py:115
  52.0 0.9 %copy.22 = bf16[32,20,9,2,4]{1,4,3,2,0:T(4,128)(2,1)S(1)} copy(bf16[32,20,9,2,4]{0,2,3,4,1:T(8,128)(2,1)S(1)} %fusion.18) | data formatting | bytes 184320 | tf_op jit(solution)/shard_map/convert_element_type | solution.py:117
  52.9 1.4 %reshape.336 = bf16[32,2,720]{2,1,0:T(2,128)(2,1)} reshape(bf16[32,9,2,4,20]{4,3,2,1,0:T(4,128)(2,1)S(1)} %bitcast.159) | data formatting | bytes 184320
  54.3 14.8 %all-to-all-start.1 = ((bf16[32,2,720]{2,1,0:T(2,128)(2,1)}), bf16[32,2,720]{2,1,0:T(2,128)(2,1)S(1)}, u32[]{:S(2)}, u32[]{:S(2)}) async-start(bf16[32,2,720]{2,1,0:T(2,128)(2,1)} %reshape.336), calls=%async_computation.1 | async-start | bytes 196608 | tf_op jit(solution)/shard_map/all_to_all | solution.py:118
  69.1 0.1 iota_compare_fusion.1
  69.2 9.8 %all-to-all-done.1 = bf16[32,2,720]{2,1,0:T(2,128)(2,1)S(1)} async-done(((bf16[32,2,720]{2,1,0:T(2,128)(2,1)}), bf16[32,2,720]{2,1,0:T(2,128)(2,1)S(1)}, u32[]{:S(2)}, u32[]{:S(2)}) %all-to-all-start.1) | async-done | bytes 92192 | tf_op jit(solution)/shard_map/all_to_all | solution.py:118
  79.0 0.4 reshape.337
  79.4 0.2 bitcast_bitcast_fusion
  79.6 0.3 copy.23
  79.9 0.5 copy.24
  80.4 2.6 %fusion.12 = bf16[20,9,2,640]{3,1,2,0:T(8,128)(2,1)S(1)} fusion(bf16[20,9,2,128]{3,1,2,0:T(8,128)(2,1)S(1)} %copy.24, bf16[20,128,640]{2,1,0:T(8,128)(2,1)} %param.11, pred[20,640]{1,0:T(8,128)(4,1)S(1)} %iota_compare_fusion.1), kind=kOutput, calls=%fused_computation.16 | convolution fusion | flops 60851200 | bytes 3842560 | tf_op jit(solution)/shard_map/sctl,sln->sctn/dot_general | solution.py:124
  82.9 1.1 %copy.25 = bf16[20,9,2,640]{3,2,1,0:T(2,128)(2,1)} copy(bf16[20,9,2,640]{3,1,2,0:T(8,128)(2,1)S(1)} %fusion.12) | data formatting | bytes 921600 | tf_op jit(solution)/shard_map/convert_element_type | solution.py:127
  (6 shorter events, 0.0 us)
Async XLA Ops:
  0.0 12.2 %collective-permute-start = (bf16[144,4,321]{2,1,0:T(4,128)(2,1)}, bf16[144,4,321]{2,1,0:T(4,128)(2,1)S(1)}, u32[]{:S(2)}, u32[]{:S(2)}) collective-permute-start(bf16[144,4,321]{2,1,0:T(4,128)(2,1)} %param.6), channel_id=1, source_target_pairs={{0,16},{16,32},{32,48},{48,64},{64,80},{80,96},{96,112},{112,128},... | collective-permute-start | bytes 1109384 | tf_op jit(solution)/shard_map/ppermute | solution.py:20
  4.0 9.6 %collective-permute-start.1 = (bf16[144,4,321]{2,1,0:T(4,128)(2,1)}, bf16[144,4,321]{2,1,0:T(4,128)(2,1)S(1)}, u32[]{:S(2)}, u32[]{:S(2)}) collective-permute-start(bf16[144,4,321]{2,1,0:T(4,128)(2,1)} %param.6), channel_id=1, source_target_pairs={{16,0},{32,16},{48,32},{64,48},{80,64},{96,80},{112,96},{128,112},... | collective-permute-start | bytes 1109384 | tf_op jit(solution)/shard_map/ppermute | solution.py:21
  20.1 27.7 %all-to-all-start = ((bf16[16,9,4,321]{3,2,1,0:T(4,128)(2,1)}), bf16[16,9,4,321]{3,2,1,0:T(4,128)(2,1)S(1)}, u32[]{:S(2)}, u32[]{:S(2)}) async-start(bf16[16,9,4,321]{3,2,1,0:T(4,128)(2,1)} %bitcast.6), calls=%async_computation | async-start | bytes 884736 | tf_op jit(solution)/shard_map/all_to_all | solution.py:89
  54.3 24.7 %all-to-all-start.1 = ((bf16[32,2,720]{2,1,0:T(2,128)(2,1)}), bf16[32,2,720]{2,1,0:T(2,128)(2,1)S(1)}, u32[]{:S(2)}, u32[]{:S(2)}) async-start(bf16[32,2,720]{2,1,0:T(2,128)(2,1)} %reshape.336), calls=%async_computation.1 | async-start | bytes 196608 | tf_op jit(solution)/shard_map/all_to_all | solution.py:118

commit v7 on v5

--- a/solution.py
+++ b/solution.py
@@ -119,6 +119,7 @@
     masked_table = jnp.where(
         degree[None, None, :] >= my_slots[:, None, None], legendre, jnp.zeros((), legendre.dtype)
     )
+    masked_table = lax.optimization_barrier(masked_table)
     result = jnp.einsum(
         "sctl,sln->sctn", sorted_waves, masked_table, preferred_element_type=jnp.float32
     )

time: 83.1 us -> 87.8 us (1.057)
  other arithmetic: 12.8 us -> 17.9 us
  local copies, waits for them, and re-layouts: 7.96 us -> 11.7 us
  waiting for transfers between devices: 23.5 us -> 21.2 us
  matrix products: 5.9 us -> 4 us
    convert_element_type x1, other arithmetic: 3.64 us -> 6.42 us  [shards(): jnp.where(inside[None], arrival, jnp.float32(0.0)).astype(jnp.bfloat16)]
    select_n x0 -> x1, other arithmetic: none -> 2.28 us  [shards(): jnp.where(degree[None, None, :] >= my_slots[:, None, None], legendre, jnp...]
    all_to_all x1, waiting for transfers between devices: 9.8 us -> 7.61 us  [shards(): lax.all_to_all(sorted_waves, LAT, split_axis=0, concat_axis=4, tiled=True)]
    dot_general x1, matrix products: 2.57 us -> 0.64 us  [shards(): jnp.einsum('sctl,sln->sctn', sorted_waves, masked_table, preferred_elemen...]
    all_to_all x2, local copies, waits for them, and re-layouts: 0.48 us -> 2.37 us  [shards(): lax.all_to_all(sorted_waves, LAT, split_axis=0, concat_axis=4, tiled=True)]
    squeeze x1, local copies, waits for them, and re-layouts: 0.45 us -> 1.5 us  [shards(): lax.all_to_all(sorted_waves, LAT, split_axis=0, concat_axis=4, tiled=True)]
    unnamed x4 -> x2, local copies, waits for them, and re-layouts: 1.74 us -> 2.55 us
  transfers between devices with their start and end apart: 4 -> 4, of which waited for: 3 -> 3; matrix products, arithmetic and copies ran while one was open for 12% -> 14% of each run, Pallas kernels for 0% -> 0%
where the time goes in v7:
time: 87.8 us; the launch traced here: 87.1 us
  starting transfers between devices  32.3 us (37%)
  waiting for transfers between devices  21.2 us (24%)
  other arithmetic  17.9 us (20%)
  local copies, waits for them, and re-layouts  11.7 us (13%)
  matrix products  4 us (5%)
    all_to_all x1, starting transfers between devices, shards(): lax.all_to_all(sorted_waves, LAT, split_axis=0, concat_axis=4, tiled=True)  14.9 us
    all_to_all x1, waiting for transfers between devices, shards(): lax.all_to_all(arrival.reshape(pieces, keep, band_rows, seg_len), 'lon',...  12.4 us
    all_to_all x1, starting transfers between devices, shards(): lax.all_to_all(arrival.reshape(pieces, keep, band_rows, seg_len), 'lon',...  12.2 us
    all_to_all x1, waiting for transfers between devices, shards(): lax.all_to_all(sorted_waves, LAT, split_axis=0, concat_axis=4, tiled=True)  7.61 us
    convert_element_type x1, other arithmetic, shards(): jnp.where(inside[None], arrival, jnp.float32(0.0)).astype(jnp.bfloat16)  6.42 us
    ppermute x1, starting transfers between devices, extended(): lax.ppermute(lax.slice_in_dim(block, block.shape[dim] - width, None, axis...  3.96 us
    another operation x1, other arithmetic  2.56 us
    unnamed x2, local copies, waits for them, and re-layouts  2.55 us
  transfers between devices with their start and end apart: 4, of which 3 were waited for; matrix products, arithmetic and copies ran while one was open for 14% of the time, Pallas kernels for 0%

profile of v7, /device:TPU:1, one launch (start us, length us, event | category | flops | bytes accessed | tf_op | source)
XLA Modules:
  0.0 87.1 jit_solution(14096182556287912000)
XLA Ops:
  0.0 1.5 %fusion.74 = (bf16[144,3,321]{2,1,0:T(4,128)(2,1)S(1)}, bf16[144,3,321]{2,1,0:T(4,128)(2,1)S(1)}) fusion(bf16[144,4,321]{2,1,0:T(4,128)(2,1)} %param.6), kind=kLoop, calls=%fused_computation.159 | loop fusion | bytes 1109376 | tf_op jit(solution)/shard_map/slice | solution.py:21
  1.5 4.0 %collective-permute-start = (bf16[144,3,321]{2,1,0:T(4,128)(2,1)S(1)}, bf16[144,3,321]{2,1,0:T(4,128)(2,1)S(1)}, u32[]{:S(2)}, u32[]{:S(2)}) collective-permute-start(bf16[144,3,321]{2,1,0:T(4,128)(2,1)S(1)} %get-tuple-element.9), channel_id=1, source_target_pairs={{0,16},{16,32},{32,48},{48,64},{64,80},{80,96},{96,112},{112,128},... | collective-permute-start | bytes 832040 | tf_op jit(solution)/shard_map/ppermute | solution.py:20
  5.5 1.3 %collective-permute-start.1 = (bf16[144,3,321]{2,1,0:T(4,128)(2,1)S(1)}, bf16[144,3,321]{2,1,0:T(4,128)(2,1)S(1)}, u32[]{:S(2)}, u32[]{:S(2)}) collective-permute-start(bf16[144,3,321]{2,1,0:T(4,128)(2,1)S(1)} %get-tuple-element.10), channel_id=1, source_target_pairs={{16,0},{32,16},{48,32},{64,48},{80,64},{96,80},{112,96},{128,112},... | collective-permute-start | bytes 832040 | tf_op jit(solution)/shard_map/ppermute | solution.py:23
  6.8 0.9 fusion.50
  7.7 0.8 fusion.54
  8.5 0.7 broadcast_divide_fusion
  9.2 0.7 convert_element_type.107
  9.9 0.1 convert_multiply_fusion.1
  10.0 0.1 convert_multiply_fusion.2
  10.0 0.7 broadcast_compare_fusion
  10.8 0.8 dynamic_slice.3
  11.5 0.1 iota_compare_fusion.1
  11.6 0.3 negate_select_fusion.4
  11.9 0.7 broadcast_compare_fusion.1
  12.6 0.8 eq.172
  13.4 0.1 copy.20
  13.5 0.3 negate_select_fusion.5
  13.8 0.0 collective-permute-done
  13.8 1.1 %collective-permute-done.1 = bf16[144,3,321]{2,1,0:T(4,128)(2,1)S(1)} collective-permute-done((bf16[144,3,321]{2,1,0:T(4,128)(2,1)S(1)}, bf16[144,3,321]{2,1,0:T(4,128)(2,1)S(1)}, u32[]{:S(2)}, u32[]{:S(2)}) %collective-permute-start.1) | collective-permute-done | bytes 277376 | tf_op jit(solution)/shard_map/ppermute | solution.py:23
  14.9 6.4 %select_convert_fusion = bf16[144,4,321]{2,1,0:T(4,128)(2,1)} fusion(bf16[144,4,321]{2,1,0:T(4,128)(2,1)} %param.6, bf16[144,3,321]{2,1,0:T(4,128)(2,1)S(1)} %collective-permute-done.1, bf16[144,3,321]{2,1,0:T(4,128)(2,1)S(1)} %collective-permute-done, f32[4,321]{1,0:T(4,128)S(1)} %get-tuple-element.23, f32[4,321]{1,0:T(4,128)S(1)} %get-tuple-element.22, ...), kind=kLoop, calls=%fused_computation.25 | loop fusion | flops 7395840 | bytes 1331508 | tf_op jit(solution)/shard_map/convert_element_type | solution.py:86
  21.3 12.2 %all-to-all-start = ((bf16[16,9,4,321]{3,2,1,0:T(4,128)(2,1)}), bf16[16,9,4,321]{3,2,1,0:T(4,128)(2,1)S(1)}, u32[]{:S(2)}, u32[]{:S(2)}) async-start(bf16[16,9,4,321]{3,2,1,0:T(4,128)(2,1)} %bitcast.6), calls=%async_computation | async-start | bytes 884736 | tf_op jit(solution)/shard_map/all_to_all | solution.py:87
  33.5 0.5 negate_select_fusion.1
  34.0 2.6 %subtract_convert_fusion = (bf16[4,11,32,640]{3,2,1,0:T(8,128)(2,1)S(1)}, bf16[4,11,32,640]{3,2,1,0:T(8,128)(2,1)}) fusion(f32[4,32,640]{2,1,0:T(8,128)S(1)} %get-tuple-element.12, f32[4,11,640]{2,1,0:T(8,128)S(1)} %get-tuple-element.16, f32[4,32,640]{2,1,0:T(8,128)S(1)} %get-tuple-element.11, f32[4,11,640]{2,1,0:T(8,128)S(1)} %get-tuple-element.15), kind=kLoop, calls=%fused_computation.1 | loop fusion | flops 8110080 | bytes 4485120 | tf_op jit(solution)/shard_map/convert.3
  36.6 12.4 %all-to-all-done = bf16[16,9,4,321]{3,2,1,0:T(4,128)(2,1)S(1)} async-done(((bf16[16,9,4,321]{3,2,1,0:T(4,128)(2,1)}), bf16[16,9,4,321]{3,2,1,0:T(4,128)(2,1)S(1)}, u32[]{:S(2)}, u32[]{:S(2)}) %all-to-all-start) | async-done | bytes 369824 | tf_op jit(solution)/shard_map/all_to_all | solution.py:87
  49.0 2.4 %fusion.1 = f32[4,16,9,1280]{3,1,2,0:T(8,128)S(1)} fusion(bf16[4,352,640]{2,1,0:T(8,128)(2,1)} %bitcast.157, bf16[4,352,640]{2,1,0:T(8,128)(2,1)S(1)} %bitcast.156, bf16[16,9,4,321]{3,2,1,0:T(4,128)(2,1)S(1)} %all-to-all-done), kind=kOutput, calls=%fused_computation.4 | convolution fusion | flops 479907840 | bytes 6923392 | tf_op jit(solution)/shard_map/pcrj,rjx->rpcx/dot_general | solution.py:93
  51.4 0.8 subtract_reduce_fusion
  52.2 1.0 %fusion.15 = bf16[32,20,9,2,4]{0,2,3,4,1:T(8,128)(2,1)S(1)} fusion(s32[32,20]{0,1:T(8,128)S(1)} %copy.20, f32[4,9,1,640]{3,1,2,0:T(8,128)S(1)} %bitcast.161, f32[4,9,1,640]{3,1,2,0:T(8,128)S(1)} %bitcast.160, f32[4]{0:T(128)S(1)} %get-tuple-element.25, pred[4,640]{1,0:T(4,128)(4,1)S(1)} %broadcast_compare_fusion), kind=kOutput, calls=%fused_computation.16 | convolution fusion | flops 59622400 | bytes 281616 | tf_op jit(solution)/shard_map/rctm,mqs->qsctr/dot_general | solution.py:113
  53.2 0.9 %copy.22 = bf16[32,20,9,2,4]{1,4,3,2,0:T(4,128)(2,1)S(1)} copy(bf16[32,20,9,2,4]{0,2,3,4,1:T(8,128)(2,1)S(1)} %fusion.15) | data formatting | bytes 184320 | tf_op jit(solution)/shard_map/convert_element_type | solution.py:115
  54.1 1.4 %reshape.336 = bf16[32,2,720]{2,1,0:T(2,128)(2,1)} reshape(bf16[32,9,2,4,20]{4,3,2,1,0:T(4,128)(2,1)S(1)} %bitcast.158) | data formatting | bytes 184320
  55.5 14.9 %all-to-all-start.1 = ((bf16[32,2,720]{2,1,0:T(2,128)(2,1)}), bf16[32,2,720]{2,1,0:T(2,128)(2,1)S(1)}, u32[]{:S(2)}, u32[]{:S(2)}) async-start(bf16[32,2,720]{2,1,0:T(2,128)(2,1)} %reshape.336), calls=%async_computation.1 | async-start | bytes 196608 | tf_op jit(solution)/shard_map/all_to_all | solution.py:116
  70.4 2.3 %broadcast_select_fusion = bf16[20,128,640]{2,1,0:T(8,128)(2,1)S(1)} fusion(bf16[20,128,640]{2,1,0:T(8,128)(2,1)} %param.11, pred[20,640]{1,0:T(8,128)(4,1)S(1)} %iota_compare_fusion.1), kind=kLoop, calls=%fused_computation.8 | loop fusion | flops 1638400 | bytes 6566400 | tf_op jit(solution)/shard_map/jit(_where)/select_n | solution.py:119
  72.6 7.6 %all-to-all-done.1 = bf16[32,2,720]{2,1,0:T(2,128)(2,1)S(1)} async-done(((bf16[32,2,720]{2,1,0:T(2,128)(2,1)}), bf16[32,2,720]{2,1,0:T(2,128)(2,1)S(1)}, u32[]{:S(2)}, u32[]{:S(2)}) %all-to-all-start.1) | async-done | bytes 92192 | tf_op jit(solution)/shard_map/all_to_all | solution.py:116
  80.3 1.2 %reshape.337 = bf16[32,9,2,4,20]{4,3,2,1,0:T(4,128)(2,1)} reshape(bf16[32,2,720]{2,1,0:T(2,128)(2,1)S(1)} %all-to-all-done.1) | data formatting | bytes 184320
  81.4 1.3 %bitcast_bitcast_fusion = bf16[1,20,9,2,32,4]{1,5,3,2,4,0:T(4,128)(2,1)S(1)} fusion(bf16[32,9,2,4,20]{4,3,2,1,0:T(4,128)(2,1)} %reshape.337), kind=kLoop, calls=%fused_computation.160 | loop fusion | bytes 184320 | tf_op jit(solution)/shard_map/all_to_all | solution.py:116
  82.7 1.1 %copy.23 = bf16[1,20,9,2,32,4]{1,5,4,3,2,0:T(4,128)(2,1)} copy(bf16[1,20,9,2,32,4]{1,5,3,2,4,0:T(4,128)(2,1)S(1)} %bitcast_bitcast_fusion) | data formatting | bytes 184320 | tf_op jit(solution)/shard_map/all_to_all | solution.py:116
  83.8 1.5 %copy.24 = bf16[20,9,2,128]{3,1,2,0:T(8,128)(2,1)S(1)} copy(bf16[20,9,2,128]{0,3,2,1:T(8,128)(2,1)} %bitcast.159) | data formatting | bytes 184320 | tf_op jit(solution)/shard_map/squeeze | solution.py:116
  85.3 0.6 fusion.9
  86.0 1.1 %copy.25 = bf16[20,9,2,640]{3,2,1,0:T(2,128)(2,1)} copy(bf16[20,9,2,640]{3,1,2,0:T(8,128)(2,1)S(1)} %fusion.9) | data formatting | bytes 921600 | tf_op jit(solution)/shard_map/convert_element_type | solution.py:126
  (6 shorter events, 0.0 us)
Async XLA Ops:
  1.5 12.3 %collective-permute-start = (bf16[144,3,321]{2,1,0:T(4,128)(2,1)S(1)}, bf16[144,3,321]{2,1,0:T(4,128)(2,1)S(1)}, u32[]{:S(2)}, u32[]{:S(2)}) collective-permute-start(bf16[144,3,321]{2,1,0:T(4,128)(2,1)S(1)} %get-tuple-element.9), channel_id=1, source_target_pairs={{0,16},{16,32},{32,48},{48,64},{64,80},{80,96},{96,112},{112,128},... | collective-permute-start | bytes 832040 | tf_op jit(solution)/shard_map/ppermute | solution.py:20
  5.5 9.4 %collective-permute-start.1 = (bf16[144,3,321]{2,1,0:T(4,128)(2,1)S(1)}, bf16[144,3,321]{2,1,0:T(4,128)(2,1)S(1)}, u32[]{:S(2)}, u32[]{:S(2)}) collective-permute-start(bf16[144,3,321]{2,1,0:T(4,128)(2,1)S(1)} %get-tuple-element.10), channel_id=1, source_target_pairs={{16,0},{32,16},{48,32},{64,48},{80,64},{96,80},{112,96},{128,112},... | collective-permute-start | bytes 832040 | tf_op jit(solution)/shard_map/ppermute | solution.py:23
  21.3 27.7 %all-to-all-start = ((bf16[16,9,4,321]{3,2,1,0:T(4,128)(2,1)}), bf16[16,9,4,321]{3,2,1,0:T(4,128)(2,1)S(1)}, u32[]{:S(2)}, u32[]{:S(2)}) async-start(bf16[16,9,4,321]{3,2,1,0:T(4,128)(2,1)} %bitcast.6), calls=%async_computation | async-start | bytes 884736 | tf_op jit(solution)/shard_map/all_to_all | solution.py:87
  55.5 24.8 %all-to-all-start.1 = ((bf16[32,2,720]{2,1,0:T(2,128)(2,1)}), bf16[32,2,720]{2,1,0:T(2,128)(2,1)S(1)}, u32[]{:S(2)}, u32[]{:S(2)}) async-start(bf16[32,2,720]{2,1,0:T(2,128)(2,1)} %reshape.336), calls=%async_computation.1 | async-start | bytes 196608 | tf_op jit(solution)/shard_map/all_to_all | solution.py:116

commit v8 on v5

--- a/solution.py
+++ b/solution.py
@@ -113,15 +113,14 @@
     sorted_waves = jnp.einsum(
         "rctm,mqs->qsctr", fourier, pick, preferred_element_type=jnp.float32
     ).astype(jnp.bfloat16)
-    sorted_waves = lax.all_to_all(sorted_waves, LAT, split_axis=0, concat_axis=4, tiled=True)[0]
+    sorted_waves = lax.all_to_all(sorted_waves, LAT, split_axis=0, concat_axis=0, tiled=True)
     my_slots = lax.dynamic_slice_in_dim(wave_order, lax.axis_index(LAT) * slots, slots)
     degree = jnp.arange(NDEG, dtype=jnp.int32)
-    masked_table = jnp.where(
-        degree[None, None, :] >= my_slots[:, None, None], legendre, jnp.zeros((), legendre.dtype)
+    table = legendre.reshape(slots, count, band_rows, NDEG)
+    result = jnp.einsum(
+        "qsctr,sqrn->sctn", sorted_waves, table, preferred_element_type=jnp.float32
     )
-    result = jnp.einsum(
-        "sctl,sln->sctn", sorted_waves, masked_table, preferred_element_type=jnp.float32
-    )
+    result = jnp.where(degree[None, None, None, :] >= my_slots[:, None, None, None], result, jnp.float32(0.0))
     return result.astype(jnp.bfloat16)
 
 

time: 83.1 us -> 90.5 us (1.089)
  local copies, waits for them, and re-layouts: 7.96 us -> 18.8 us
  starting transfers between devices: 32.3 us -> 28.2 us
  other arithmetic: 12.8 us -> 14.2 us
  waiting for transfers between devices: 23.5 us -> 22.2 us
    reshape x0 -> x1, local copies, waits for them, and re-layouts: none -> 6.56 us  [shards(): table = legendre.reshape(slots, count, band_rows, NDEG)]
    all_to_all x1, starting transfers between devices: 12.2 us -> 8.07 us  [shards(): lax.all_to_all(arrival.reshape(pieces, keep, band_rows, seg_len), 'lon',...]
    all_to_all x2 -> x1, local copies, waits for them, and re-layouts: 0.48 us -> 3 us  [shards(): lax.all_to_all(sorted_waves, LAT, split_axis=0, concat_axis=0, tiled=True)]
    unnamed x4 -> x6, local copies, waits for them, and re-layouts: 1.74 us -> 3.57 us
    convert_element_type x1, local copies, waits for them, and re-layouts: 0.94 us -> 2.44 us  [shards(): sorted_waves = jnp.einsum('rctm,mqs->qsctr', fourier, pick, preferred_ele...]
    convert_element_type x0 -> x2, other arithmetic: none -> 1.32 us  [the longest x1 1.21 us: shards(): return result.astype(jnp.bfloat16)]
    ppermute x1, waiting for transfers between devices: 1.21 us -> 0.01 us  [extended(): lax.ppermute(lax.slice_in_dim(block, 0, width, axis=dim), axis, backward)]
    convert_element_type x1 -> x0, local copies, waits for them, and re-layouts: 1.14 us -> none  [shards(): return result.astype(jnp.bfloat16)]
  transfers between devices with their start and end apart: 4 -> 4, of which waited for: 3 -> 2; matrix products, arithmetic and copies ran while one was open for 12% -> 18% of each run, Pallas kernels for 0% -> 0%
where the time goes in v8:
time: 90.5 us; the launch traced here: 89.7 us
  starting transfers between devices  28.2 us (31%)
  waiting for transfers between devices  22.2 us (25%)
  local copies, waits for them, and re-layouts  18.8 us (21%)
  other arithmetic  14.2 us (16%)
  matrix products  6.19 us (7%)
    all_to_all x1, starting transfers between devices, shards(): lax.all_to_all(sorted_waves, LAT, split_axis=0, concat_axis=0, tiled=True)  14.8 us
    all_to_all x1, waiting for transfers between devices, shards(): lax.all_to_all(arrival.reshape(pieces, keep, band_rows, seg_len), 'lon',...  12.4 us
    all_to_all x1, waiting for transfers between devices, shards(): lax.all_to_all(sorted_waves, LAT, split_axis=0, concat_axis=0, tiled=True)  9.82 us
    all_to_all x1, starting transfers between devices, shards(): lax.all_to_all(arrival.reshape(pieces, keep, band_rows, seg_len), 'lon',...  8.07 us
    reshape x1, local copies, waits for them, and re-layouts, shards(): table = legendre.reshape(slots, count, band_rows, NDEG)  6.56 us
    ppermute x1, starting transfers between devices, extended(): lax.ppermute(lax.slice_in_dim(block, block.shape[dim] - width, None, axis...  3.96 us
    convert_element_type x1, other arithmetic, shards(): jnp.where(inside[None], arrival, jnp.float32(0.0)).astype(jnp.bfloat16)  3.66 us
    unnamed x6, local copies, waits for them, and re-layouts  3.57 us
  transfers between devices with their start and end apart: 4, of which 2 were waited for; matrix products, arithmetic and copies ran while one was open for 18% of the time, Pallas kernels for 0%

profile of v8, /device:TPU:1, one launch (start us, length us, event | category | flops | bytes accessed | tf_op | source)
XLA Modules:
  0.0 89.7 jit_solution(9929554241031441468)
XLA Ops:
  0.0 1.5 %fusion.70 = (bf16[144,3,321]{2,1,0:T(4,128)(2,1)S(1)}, bf16[144,3,321]{2,1,0:T(4,128)(2,1)S(1)}) fusion(bf16[144,4,321]{2,1,0:T(4,128)(2,1)} %param.6), kind=kLoop, calls=%fused_computation.158 | loop fusion | bytes 1109376 | tf_op jit(solution)/shard_map/slice | solution.py:21
  1.5 4.0 %collective-permute-start = (bf16[144,3,321]{2,1,0:T(4,128)(2,1)S(1)}, bf16[144,3,321]{2,1,0:T(4,128)(2,1)S(1)}, u32[]{:S(2)}, u32[]{:S(2)}) collective-permute-start(bf16[144,3,321]{2,1,0:T(4,128)(2,1)S(1)} %get-tuple-element.9), channel_id=1, source_target_pairs={{0,16},{16,32},{32,48},{48,64},{64,80},{80,96},{96,112},{112,128},... | collective-permute-start | bytes 832040 | tf_op jit(solution)/shard_map/ppermute | solution.py:20
  5.5 1.3 %collective-permute-start.1 = (bf16[144,3,321]{2,1,0:T(4,128)(2,1)S(1)}, bf16[144,3,321]{2,1,0:T(4,128)(2,1)S(1)}, u32[]{:S(2)}, u32[]{:S(2)}) collective-permute-start(bf16[144,3,321]{2,1,0:T(4,128)(2,1)S(1)} %get-tuple-element.10), channel_id=1, source_target_pairs={{16,0},{32,16},{48,32},{64,48},{80,64},{96,80},{112,96},{128,112},... | collective-permute-start | bytes 832040 | tf_op jit(solution)/shard_map/ppermute | solution.py:23
  6.8 0.9 fusion.48
  7.7 0.8 fusion.52
  8.5 0.7 broadcast_divide_fusion
  9.2 0.7 convert_element_type.107
  9.9 0.1 convert_multiply_fusion.1
  10.0 0.1 convert_multiply_fusion.2
  10.0 0.7 broadcast_compare_fusion
  10.8 0.3 negate_select_fusion.4
  11.0 0.7 broadcast_compare_fusion.1
  11.8 0.8 eq.172
  12.6 0.1 copy.31
  12.6 0.0 copy-start
  12.6 6.6 %reshape.334 = bf16[20,32,4,640]{3,2,1,0:T(4,128)(2,1)} reshape(bf16[20,128,640]{2,1,0:T(8,128)(2,1)} %param.11) | data formatting | bytes 6553600 | tf_op jit(solution)/shard_map/reshape | solution.py:119
  19.2 0.8 dynamic_slice.3
  20.0 0.3 negate_select_fusion.5
  20.3 0.0 collective-permute-done
  20.3 0.0 collective-permute-done.1
  20.3 0.0 copy-done
  20.3 3.7 %select_convert_fusion = bf16[144,4,321]{2,1,0:T(4,128)(2,1)} fusion(bf16[144,4,321]{2,1,0:T(4,128)(2,1)S(1)} %copy-done, bf16[144,3,321]{2,1,0:T(4,128)(2,1)S(1)} %collective-permute-done.1, bf16[144,3,321]{2,1,0:T(4,128)(2,1)S(1)} %collective-permute-done, f32[4,321]{1,0:T(4,128)S(1)} %get-tuple-element.23, f32[4,321]{1,0:T(4,128)S(1)} %get-tuple-element.22, ...), kind=kLoop, calls=%fused_computation.26 | loop fusion | flops 7395840 | bytes 1331508 | tf_op jit(solution)/shard_map/convert_element_type | solution.py:86
  23.9 8.1 %all-to-all-start = ((bf16[16,9,4,321]{3,2,1,0:T(4,128)(2,1)}), bf16[16,9,4,321]{3,2,1,0:T(4,128)(2,1)S(1)}, u32[]{:S(2)}, u32[]{:S(2)}) async-start(bf16[16,9,4,321]{3,2,1,0:T(4,128)(2,1)} %bitcast.6), calls=%async_computation | async-start | bytes 884736 | tf_op jit(solution)/shard_map/all_to_all | solution.py:87
  32.0 0.5 negate_select_fusion.1
  32.5 2.6 %subtract_convert_fusion = (bf16[4,11,32,640]{3,2,1,0:T(8,128)(2,1)S(1)}, bf16[4,11,32,640]{3,2,1,0:T(8,128)(2,1)}) fusion(f32[4,32,640]{2,1,0:T(8,128)S(1)} %get-tuple-element.12, f32[4,11,640]{2,1,0:T(8,128)S(1)} %get-tuple-element.16, f32[4,32,640]{2,1,0:T(8,128)S(1)} %get-tuple-element.11, f32[4,11,640]{2,1,0:T(8,128)S(1)} %get-tuple-element.15), kind=kLoop, calls=%fused_computation.1 | loop fusion | flops 8110080 | bytes 4485120 | tf_op jit(solution)/shard_map/convert.3
  35.1 12.4 %all-to-all-done = bf16[16,9,4,321]{3,2,1,0:T(4,128)(2,1)S(1)} async-done(((bf16[16,9,4,321]{3,2,1,0:T(4,128)(2,1)}), bf16[16,9,4,321]{3,2,1,0:T(4,128)(2,1)S(1)}, u32[]{:S(2)}, u32[]{:S(2)}) %all-to-all-start) | async-done | bytes 369824 | tf_op jit(solution)/shard_map/all_to_all | solution.py:87
  47.5 2.4 %fusion.1 = f32[4,16,9,1280]{3,1,2,0:T(8,128)S(1)} fusion(bf16[4,352,640]{2,1,0:T(8,128)(2,1)} %bitcast.150, bf16[4,352,640]{2,1,0:T(8,128)(2,1)S(1)} %bitcast.149, bf16[16,9,4,321]{3,2,1,0:T(4,128)(2,1)S(1)} %all-to-all-done), kind=kOutput, calls=%fused_computation.4 | convolution fusion | flops 479907840 | bytes 6923392 | tf_op jit(solution)/shard_map/pcrj,rjx->rpcx/dot_general | solution.py:93
  49.9 0.8 subtract_reduce_fusion
  50.7 0.1 copy_bitcast_fusion
  50.8 0.1 fusion.32
  50.9 0.0 copy-start.1
  50.9 1.8 %fusion.15 = bf16[32,20,9,2,4]{0,2,4,3,1:T(8,128)(2,1)} fusion(s32[32,20]{0,1:T(8,128)S(1)} %copy.31, bf16[4,9,2,640]{3,0,1,2:T(4,128)(2,1)S(1)} %fusion.32), kind=kOutput, calls=%fused_computation.15 | convolution fusion | flops 59438080 | bytes 186880 | tf_op jit(solution)/shard_map/rctm,mqs->qsctr/dot_general | solution.py:113
  52.7 2.4 %copy.36 = bf16[32,20,9,2,4]{1,4,3,2,0:T(4,128)(2,1)} copy(bf16[32,20,9,2,4]{0,2,4,3,1:T(8,128)(2,1)} %fusion.15) | data formatting | bytes 184320 | tf_op jit(solution)/shard_map/convert_element_type | solution.py:115
  55.2 2.4 %reshape.340 = bf16[32,2,720]{2,1,0:T(2,128)(2,1)} reshape(bf16[32,9,2,4,20]{4,3,2,1,0:T(4,128)(2,1)} %bitcast.152) | data formatting | bytes 184320
  57.5 14.8 %all-to-all-start.1 = ((bf16[32,2,720]{2,1,0:T(2,128)(2,1)}), bf16[32,2,720]{2,1,0:T(2,128)(2,1)S(1)}, u32[]{:S(2)}, u32[]{:S(2)}) async-start(bf16[32,2,720]{2,1,0:T(2,128)(2,1)} %reshape.340), calls=%async_computation.1 | async-start | bytes 196608 | tf_op jit(solution)/shard_map/all_to_all | solution.py:116
  72.4 0.1 iota_compare_fusion.1
  72.5 9.8 %all-to-all-done.1 = bf16[32,2,720]{2,1,0:T(2,128)(2,1)S(1)} async-done(((bf16[32,2,720]{2,1,0:T(2,128)(2,1)}), bf16[32,2,720]{2,1,0:T(2,128)(2,1)S(1)}, u32[]{:S(2)}, u32[]{:S(2)}) %all-to-all-start.1) | async-done | bytes 92192 | tf_op jit(solution)/shard_map/all_to_all | solution.py:116
  82.3 1.2 %reshape.341 = bf16[32,9,2,4,20]{4,3,2,1,0:T(4,128)(2,1)} reshape(bf16[32,2,720]{2,1,0:T(2,128)(2,1)S(1)} %all-to-all-done.1) | data formatting | bytes 184320
  83.5 3.0 %copy.37 = bf16[32,20,9,2,4]{0,2,4,3,1:T(8,128)(2,1)} copy(bf16[32,20,9,2,4]{1,4,3,2,0:T(4,128)(2,1)} %bitcast.153) | data formatting | bytes 184320 | tf_op jit(solution)/shard_map/all_to_all | solution.py:116
  86.5 0.0 copy-done.1
  86.5 2.0 %fusion.9 = bf16[20,9,2,640]{3,1,2,0:T(8,128)(2,1)S(1)} fusion(bf16[32,20,9,2,4]{0,2,4,3,1:T(8,128)(2,1)} %copy.37, bf16[20,32,4,640,1]{3,2,1,0,4:T(4,128)(2,1)S(1)} %bitcast.151), kind=kOutput, calls=%fused_computation.11 | convolution fusion | flops 58982400 | bytes 3829760 | tf_op jit(solution)/shard_map/qsctr,sqrn->sctn/dot_general | solution.py:120
  88.5 1.2 %fusion.18 = bf16[20,9,2,640]{3,2,1,0:T(2,128)(2,1)} fusion(bf16[20,9,2,640]{3,1,2,0:T(8,128)(2,1)S(1)} %fusion.9, pred[20,640]{1,0:T(8,128)(4,1)S(1)} %iota_compare_fusion.1), kind=kLoop, calls=%fused_computation.25 | loop fusion | flops 230400 | bytes 934400 | tf_op jit(solution)/shard_map/convert_element_type | solution.py:124
  (6 shorter events, 0.0 us)
Async XLA Ops:
  1.5 18.7 %collective-permute-start = (bf16[144,3,321]{2,1,0:T(4,128)(2,1)S(1)}, bf16[144,3,321]{2,1,0:T(4,128)(2,1)S(1)}, u32[]{:S(2)}, u32[]{:S(2)}) collective-permute-start(bf16[144,3,321]{2,1,0:T(4,128)(2,1)S(1)} %get-tuple-element.9), channel_id=1, source_target_pairs={{0,16},{16,32},{32,48},{48,64},{64,80},{80,96},{96,112},{112,128},... | collective-permute-start | bytes 832040 | tf_op jit(solution)/shard_map/ppermute | solution.py:20
  5.5 14.8 %collective-permute-start.1 = (bf16[144,3,321]{2,1,0:T(4,128)(2,1)S(1)}, bf16[144,3,321]{2,1,0:T(4,128)(2,1)S(1)}, u32[]{:S(2)}, u32[]{:S(2)}) collective-permute-start(bf16[144,3,321]{2,1,0:T(4,128)(2,1)S(1)} %get-tuple-element.10), channel_id=1, source_target_pairs={{16,0},{32,16},{48,32},{64,48},{80,64},{96,80},{112,96},{128,112},... | collective-permute-start | bytes 832040 | tf_op jit(solution)/shard_map/ppermute | solution.py:23
  12.6 7.6 %copy-start = (bf16[144,4,321]{2,1,0:T(4,128)(2,1)S(1)}, bf16[144,4,321]{2,1,0:T(4,128)(2,1)}, u32[]{:S(2)}) copy-start(bf16[144,4,321]{2,1,0:T(4,128)(2,1)} %param.6) | copy-start | bytes 1109380
  23.9 23.6 %all-to-all-start = ((bf16[16,9,4,321]{3,2,1,0:T(4,128)(2,1)}), bf16[16,9,4,321]{3,2,1,0:T(4,128)(2,1)S(1)}, u32[]{:S(2)}, u32[]{:S(2)}) async-start(bf16[16,9,4,321]{3,2,1,0:T(4,128)(2,1)} %bitcast.6), calls=%async_computation | async-start | bytes 884736 | tf_op jit(solution)/shard_map/all_to_all | solution.py:87
  50.9 35.6 %copy-start.1 = (bf16[20,32,4,640]{3,2,1,0:T(4,128)(2,1)S(1)}, bf16[20,32,4,640]{3,2,1,0:T(4,128)(2,1)}, u32[]{:S(2)}) copy-start(bf16[20,32,4,640]{3,2,1,0:T(4,128)(2,1)} %reshape.334) | copy-start | bytes 9830404
  57.5 24.7 %all-to-all-start.1 = ((bf16[32,2,720]{2,1,0:T(2,128)(2,1)}), bf16[32,2,720]{2,1,0:T(2,128)(2,1)S(1)}, u32[]{:S(2)}, u32[]{:S(2)}) async-start(bf16[32,2,720]{2,1,0:T(2,128)(2,1)} %reshape.340), calls=%async_computation.1 | async-start | bytes 196608 | tf_op jit(solution)/shard_map/all_to_all | solution.py:116

commit v9 on v5

--- a/solution.py
+++ b/solution.py
@@ -90,6 +90,11 @@
     tables = segment_tables(row_points, seg_len, M)
     starts = jnp.arange(pieces, dtype=jnp.int32) * seg_len
     phase_re, phase_im = phase_pair(row_points, starts, M)
+    wavenumber = jnp.arange(M, dtype=jnp.int32)
+    inverse = jnp.float32(1.0) / row_points.astype(jnp.float32)
+    resolved = 2 * wavenumber[None, :] < row_points[:, None]
+    scale = jnp.where(resolved, inverse[:, None], jnp.float32(0.0))[:, None, :]
+    phase_re, phase_im = phase_re * scale, phase_im * scale
     spectra = jnp.einsum(
         "pcrj,rjx->rpcx", gathered, tables, preferred_element_type=jnp.float32
     )
@@ -100,14 +105,7 @@
     imag_part = jnp.sum(
         phase_re[:, :, None, :] * spectra_im + phase_im[:, :, None, :] * spectra_re, axis=1
     )
-    fourier = jnp.stack([real_part, imag_part], axis=2)
-    wavenumber = jnp.arange(M, dtype=jnp.int32)
-    inverse = jnp.float32(1.0) / row_points.astype(jnp.float32)
-    resolved = 2 * wavenumber[None, :] < row_points[:, None]
-    fourier = jnp.where(
-        resolved[:, None, None, :], fourier * inverse[:, None, None, None], jnp.float32(0.0)
-    )
-    fourier = fourier.astype(jnp.bfloat16)
+    fourier = jnp.stack([real_part, imag_part], axis=2).astype(jnp.bfloat16)
     count = lax.axis_size(LAT)
     pick = (wave_order[None, :] == wavenumber[:, None]).astype(jnp.bfloat16).reshape(M, count, slots)
     sorted_waves = jnp.einsum(

time: 83.1 us -> 83.2 us (level)
  no operation moved by 1% of the time
where the time goes in v9:
time: 83.2 us; the launch traced here: 82.6 us
  starting transfers between devices  32.3 us (39%)
  waiting for transfers between devices  23.5 us (28%)
  other arithmetic  12.8 us (15%)
  local copies, waits for them, and re-layouts  7.96 us (10%)
  matrix products  5.92 us (7%)
    all_to_all x1, starting transfers between devices, shards(): lax.all_to_all(sorted_waves, LAT, split_axis=0, concat_axis=4, tiled=True)  14.9 us
    all_to_all x1, waiting for transfers between devices, shards(): lax.all_to_all(arrival.reshape(pieces, keep, band_rows, seg_len), 'lon',...  12.4 us
    all_to_all x1, starting transfers between devices, shards(): lax.all_to_all(arrival.reshape(pieces, keep, band_rows, seg_len), 'lon',...  12.2 us
    all_to_all x1, waiting for transfers between devices, shards(): lax.all_to_all(sorted_waves, LAT, split_axis=0, concat_axis=4, tiled=True)  9.82 us
    ppermute x1, starting transfers between devices, extended(): lax.ppermute(lax.slice_in_dim(block, block.shape[dim] - width, None, axis...  3.96 us
    convert_element_type x1, other arithmetic, shards(): jnp.where(inside[None], arrival, jnp.float32(0.0)).astype(jnp.bfloat16)  3.64 us
    dot_general x1, matrix products, shards(): jnp.einsum('sctl,sln->sctn', sorted_waves, masked_table, preferred_elemen...  2.57 us
    another operation x1, other arithmetic  2.56 us
  transfers between devices with their start and end apart: 4, of which 3 were waited for; matrix products, arithmetic and copies ran while one was open for 12% of the time, Pallas kernels for 0%

profile of v9, /device:TPU:1, one launch (start us, length us, event | category | flops | bytes accessed | tf_op | source)
XLA Modules:
  0.0 82.6 jit_solution(4765647649124388069)
XLA Ops:
  0.0 0.0 copy-start
  0.0 1.6 %fusion.74 = (bf16[144,3,321]{2,1,0:T(4,128)(2,1)S(1)}, bf16[144,3,321]{2,1,0:T(4,128)(2,1)S(1)}) fusion(bf16[144,4,321]{2,1,0:T(4,128)(2,1)} %param.6), kind=kLoop, calls=%fused_computation.161 | loop fusion | bytes 1109376 | tf_op jit(solution)/shard_map/slice | solution.py:21
  1.6 4.0 %collective-permute-start = (bf16[144,3,321]{2,1,0:T(4,128)(2,1)S(1)}, bf16[144,3,321]{2,1,0:T(4,128)(2,1)S(1)}, u32[]{:S(2)}, u32[]{:S(2)}) collective-permute-start(bf16[144,3,321]{2,1,0:T(4,128)(2,1)S(1)} %get-tuple-element.9), channel_id=1, source_target_pairs={{0,16},{16,32},{32,48},{48,64},{64,80},{80,96},{96,112},{112,128},... | collective-permute-start | bytes 832040 | tf_op jit(solution)/shard_map/ppermute | solution.py:20
  5.6 1.3 %collective-permute-start.1 = (bf16[144,3,321]{2,1,0:T(4,128)(2,1)S(1)}, bf16[144,3,321]{2,1,0:T(4,128)(2,1)S(1)}, u32[]{:S(2)}, u32[]{:S(2)}) collective-permute-start(bf16[144,3,321]{2,1,0:T(4,128)(2,1)S(1)} %get-tuple-element.10), channel_id=1, source_target_pairs={{16,0},{32,16},{48,32},{64,48},{80,64},{96,80},{112,96},{128,112},... | collective-permute-start | bytes 832040 | tf_op jit(solution)/shard_map/ppermute | solution.py:23
  6.9 0.9 %fusion.50 = (f32[4,321]{1,0:T(4,128)S(1)}, f32[4,321]{1,0:T(4,128)S(1)}, f32[4,321]{1,0:T(4,128)S(1)}, f32[4,321]{1,0:T(4,128)S(1)}) fusion(f32[4,4,321]{2,1,0:T(4,128)} %param.7, s32[4,321]{1,0:T(4,128)} %param.8, s32[4]{0:T(128)S(1)} %iota_add_fusion.1), kind=kLoop, calls=%fused_computation.104 | loop fusion | flops 61632 | bytes 46240 | tf_op jit(solution)/shard_map/add | solution.py:79
  7.7 0.8 %fusion.54 = (f32[4,321]{1,0:T(4,128)S(1)}, f32[4,321]{1,0:T(4,128)S(1)}, f32[4,321]{1,0:T(4,128)S(1)}) fusion(f32[4,4,321]{2,1,0:T(4,128)} %param.7, s32[4,321]{1,0:T(4,128)} %param.8, s32[4]{0:T(128)S(1)} %iota_add_fusion.1), kind=kLoop, calls=%fused_computation.108 | loop fusion | flops 47508 | bytes 41104 | tf_op jit(solution)/shard_map/add | solution.py:79
  8.6 0.7 broadcast_divide_fusion
  9.2 0.7 convert_element_type.105
  9.9 0.1 convert_multiply_fusion.1
  10.0 0.1 convert_multiply_fusion.2
  10.1 0.7 compare_select_fusion
  10.8 0.3 negate_select_fusion.4
  11.1 0.7 broadcast_compare_fusion
  11.8 0.8 eq.172
  12.6 0.1 copy.20
  12.7 0.8 dynamic_slice.3
  13.5 0.3 fusion.33
  13.8 0.0 collective-permute-done
  13.8 1.2 %collective-permute-done.1 = bf16[144,3,321]{2,1,0:T(4,128)(2,1)S(1)} collective-permute-done((bf16[144,3,321]{2,1,0:T(4,128)(2,1)S(1)}, bf16[144,3,321]{2,1,0:T(4,128)(2,1)S(1)}, u32[]{:S(2)}, u32[]{:S(2)}) %collective-permute-start.1) | collective-permute-done | bytes 277376 | tf_op jit(solution)/shard_map/ppermute | solution.py:23
  15.0 0.0 copy-done
  15.0 3.6 %select_convert_fusion = bf16[144,4,321]{2,1,0:T(4,128)(2,1)} fusion(bf16[144,4,321]{2,1,0:T(4,128)(2,1)S(1)} %copy-done, bf16[144,3,321]{2,1,0:T(4,128)(2,1)S(1)} %collective-permute-done.1, bf16[144,3,321]{2,1,0:T(4,128)(2,1)S(1)} %collective-permute-done, f32[4,321]{1,0:T(4,128)S(1)} %get-tuple-element.23, f32[4,321]{1,0:T(4,128)S(1)} %get-tuple-element.22, ...), kind=kLoop, calls=%fused_computation.27 | loop fusion | flops 7395840 | bytes 1331508 | tf_op jit(solution)/shard_map/convert_element_type | solution.py:86
  18.6 12.2 %all-to-all-start = ((bf16[16,9,4,321]{3,2,1,0:T(4,128)(2,1)}), bf16[16,9,4,321]{3,2,1,0:T(4,128)(2,1)S(1)}, u32[]{:S(2)}, u32[]{:S(2)}) async-start(bf16[16,9,4,321]{3,2,1,0:T(4,128)(2,1)} %bitcast.6), calls=%async_computation | async-start | bytes 884736 | tf_op jit(solution)/shard_map/all_to_all | solution.py:87
  30.8 0.5 negate_select_fusion.1
  31.3 2.6 %subtract_convert_fusion = (bf16[4,11,32,640]{3,2,1,0:T(8,128)(2,1)S(1)}, bf16[4,11,32,640]{3,2,1,0:T(8,128)(2,1)}) fusion(f32[4,32,640]{2,1,0:T(8,128)S(1)} %get-tuple-element.12, f32[4,11,640]{2,1,0:T(8,128)S(1)} %get-tuple-element.16, f32[4,32,640]{2,1,0:T(8,128)S(1)} %get-tuple-element.11, f32[4,11,640]{2,1,0:T(8,128)S(1)} %get-tuple-element.15), kind=kLoop, calls=%fused_computation.1 | loop fusion | flops 8110080 | bytes 4485120 | tf_op jit(solution)/shard_map/convert.7
  33.9 12.4 %all-to-all-done = bf16[16,9,4,321]{3,2,1,0:T(4,128)(2,1)S(1)} async-done(((bf16[16,9,4,321]{3,2,1,0:T(4,128)(2,1)}), bf16[16,9,4,321]{3,2,1,0:T(4,128)(2,1)S(1)}, u32[]{:S(2)}, u32[]{:S(2)}) %all-to-all-start) | async-done | bytes 369824 | tf_op jit(solution)/shard_map/all_to_all | solution.py:87
  46.3 2.4 %fusion.1 = f32[4,16,9,1280]{3,1,2,0:T(8,128)S(1)} fusion(bf16[4,352,640]{2,1,0:T(8,128)(2,1)} %bitcast.161, bf16[4,352,640]{2,1,0:T(8,128)(2,1)S(1)} %bitcast.160, bf16[16,9,4,321]{3,2,1,0:T(4,128)(2,1)S(1)} %all-to-all-done), kind=kOutput, calls=%fused_computation.4 | convolution fusion | flops 479907840 | bytes 6923392 | tf_op jit(solution)/shard_map/pcrj,rjx->rpcx/dot_general | solution.py:98
  48.7 0.8 subtract_reduce_fusion
  49.5 1.0 %fusion.18 = bf16[32,20,9,2,4]{0,2,3,4,1:T(8,128)(2,1)S(1)} fusion(s32[32,20]{0,1:T(8,128)S(1)} %copy.20, bf16[4,9,1,640]{3,1,2,0:T(8,128)(2,1)S(1)} %bitcast.165, bf16[4,9,1,640]{3,1,2,0:T(8,128)(2,1)S(1)} %bitcast.164), kind=kOutput, calls=%fused_computation.18 | convolution fusion | flops 59622400 | bytes 186880 | tf_op jit(solution)/shard_map/rctm,mqs->qsctr/dot_general | solution.py:111
  50.5 0.9 %copy.22 = bf16[32,20,9,2,4]{1,4,3,2,0:T(4,128)(2,1)S(1)} copy(bf16[32,20,9,2,4]{0,2,3,4,1:T(8,128)(2,1)S(1)} %fusion.18) | data formatting | bytes 184320 | tf_op jit(solution)/shard_map/convert_element_type | solution.py:113
  51.4 1.4 %reshape.349 = bf16[32,2,720]{2,1,0:T(2,128)(2,1)} reshape(bf16[32,9,2,4,20]{4,3,2,1,0:T(4,128)(2,1)S(1)} %bitcast.162) | data formatting | bytes 184320
  52.8 14.9 %all-to-all-start.1 = ((bf16[32,2,720]{2,1,0:T(2,128)(2,1)}), bf16[32,2,720]{2,1,0:T(2,128)(2,1)S(1)}, u32[]{:S(2)}, u32[]{:S(2)}) async-start(bf16[32,2,720]{2,1,0:T(2,128)(2,1)} %reshape.349), calls=%async_computation.1 | async-start | bytes 196608 | tf_op jit(solution)/shard_map/all_to_all | solution.py:114
  67.7 0.1 iota_compare_fusion.1
  67.7 9.8 %all-to-all-done.1 = bf16[32,2,720]{2,1,0:T(2,128)(2,1)S(1)} async-done(((bf16[32,2,720]{2,1,0:T(2,128)(2,1)}), bf16[32,2,720]{2,1,0:T(2,128)(2,1)S(1)}, u32[]{:S(2)}, u32[]{:S(2)}) %all-to-all-start.1) | async-done | bytes 92192 | tf_op jit(solution)/shard_map/all_to_all | solution.py:114
  77.6 0.4 reshape.350
  77.9 0.2 bitcast_bitcast_fusion
  78.2 0.3 copy.23
  78.4 0.5 copy.24
  78.9 2.6 %fusion.12 = bf16[20,9,2,640]{3,1,2,0:T(8,128)(2,1)S(1)} fusion(bf16[20,9,2,128]{3,1,2,0:T(8,128)(2,1)S(1)} %copy.24, bf16[20,128,640]{2,1,0:T(8,128)(2,1)} %param.11, pred[20,640]{1,0:T(8,128)(4,1)S(1)} %iota_compare_fusion.1), kind=kOutput, calls=%fused_computation.16 | convolution fusion | flops 60851200 | bytes 3842560 | tf_op jit(solution)/shard_map/sctl,sln->sctn/dot_general | solution.py:120
  81.5 1.1 %copy.25 = bf16[20,9,2,640]{3,2,1,0:T(2,128)(2,1)} copy(bf16[20,9,2,640]{3,1,2,0:T(8,128)(2,1)S(1)} %fusion.12) | data formatting | bytes 921600 | tf_op jit(solution)/shard_map/convert_element_type | solution.py:123
  (6 shorter events, 0.0 us)
Async XLA Ops:
  0.0 15.0 %copy-start = (bf16[144,4,321]{2,1,0:T(4,128)(2,1)S(1)}, bf16[144,4,321]{2,1,0:T(4,128)(2,1)}, u32[]{:S(2)}) copy-start(bf16[144,4,321]{2,1,0:T(4,128)(2,1)} %param.6) | copy-start | bytes 1109380
  1.6 12.2 %collective-permute-start = (bf16[144,3,321]{2,1,0:T(4,128)(2,1)S(1)}, bf16[144,3,321]{2,1,0:T(4,128)(2,1)S(1)}, u32[]{:S(2)}, u32[]{:S(2)}) collective-permute-start(bf16[144,3,321]{2,1,0:T(4,128)(2,1)S(1)} %get-tuple-element.9), channel_id=1, source_target_pairs={{0,16},{16,32},{32,48},{48,64},{64,80},{80,96},{96,112},{112,128},... | collective-permute-start | bytes 832040 | tf_op jit(solution)/shard_map/ppermute | solution.py:20
  5.6 9.4 %collective-permute-start.1 = (bf16[144,3,321]{2,1,0:T(4,128)(2,1)S(1)}, bf16[144,3,321]{2,1,0:T(4,128)(2,1)S(1)}, u32[]{:S(2)}, u32[]{:S(2)}) collective-permute-start(bf16[144,3,321]{2,1,0:T(4,128)(2,1)S(1)} %get-tuple-element.10), channel_id=1, source_target_pairs={{16,0},{32,16},{48,32},{64,48},{80,64},{96,80},{112,96},{128,112},... | collective-permute-start | bytes 832040 | tf_op jit(solution)/shard_map/ppermute | solution.py:23
  18.6 27.7 %all-to-all-start = ((bf16[16,9,4,321]{3,2,1,0:T(4,128)(2,1)}), bf16[16,9,4,321]{3,2,1,0:T(4,128)(2,1)S(1)}, u32[]{:S(2)}, u32[]{:S(2)}) async-start(bf16[16,9,4,321]{3,2,1,0:T(4,128)(2,1)} %bitcast.6), calls=%async_computation | async-start | bytes 884736 | tf_op jit(solution)/shard_map/all_to_all | solution.py:87
  52.8 24.8 %all-to-all-start.1 = ((bf16[32,2,720]{2,1,0:T(2,128)(2,1)}), bf16[32,2,720]{2,1,0:T(2,128)(2,1)S(1)}, u32[]{:S(2)}, u32[]{:S(2)}) async-start(bf16[32,2,720]{2,1,0:T(2,128)(2,1)} %reshape.349), calls=%async_computation.1 | async-start | bytes 196608 | tf_op jit(solution)/shard_map/all_to_all | solution.py:114
